TPU v7x, 768 devices: a whole 4x8x12 slice. The times are simulated.
768 devices in a mesh: dp: 128 (over y, x, z_hi, core), space: 6 (over z_lo).
Axes of the slice: x: 4, y: 8, z: 12 (z_hi: 2, z_lo: 6; z = z_hi * 6 + z_lo), core: 2. Of those that a mesh axis runs over, the one named last changes fastest.
Arguments:
- activations: bfloat16 [128, 32, 24, 256], P('dp', None, 'space'), may hold values from -6 to 6
- cotangent: bfloat16 [128, 128, 12, 64], P('dp', None, 'space'), may hold values from -12 to 12
- weight_mid: bfloat16 [3, 3, 3, 32, 64], replicated, may hold values from -0.21875 to 0.21875
- weight_deep: bfloat16 [3, 3, 3, 64, 128], replicated, may hold values from -0.15625 to 0.15625
Outputs:
- grad_input: bfloat16 [128, 32, 24, 256], P('dp', None, 'space')
- grad_mid: float32 [3, 3, 3, 32, 64], replicated
- grad_deep: float32 [3, 3, 3, 64, 128], replicated
All inputs are finite; a program needn't handle non-finite values.
Results may differ from a plain program's by a relative error of at most 0.0059.
Values may be sent and summed in bfloat16 or wider, within the bound.
No kernel may reach another device: no remote copies, remote signals or barrier semaphores. Data moves between devices by JAX's collectives and lax.ppermute only.
A program may use at most 32 MiB of HBM per device.

v0:
```python
import jax
import jax.numpy as jnp
from jax import lax
from jax.sharding import Mesh, PartitionSpec as P

ROWS = 4
COLS = 64


def extended(block, sides, width):
    for axis, dim in sides:
        count = lax.axis_size(axis)
        forward = [(i, i + 1) for i in range(count - 1)]
        backward = [(target, source) for source, target in forward]
        low = lax.ppermute(
            lax.slice_in_dim(block, block.shape[dim] - width, None, axis=dim), axis, forward
        )
        high = lax.ppermute(lax.slice_in_dim(block, 0, width, axis=dim), axis, backward)
        block = jnp.concatenate([low, block, high], axis=dim)
    return block


def shifted(planes, row_step, col_step, row_count, col_count):
    margin = col_count + 1
    widened = jnp.pad(planes, ((0, 0), (0, 0), (margin, margin)))
    offset = margin + row_step * col_count + col_step
    moved_cells = widened[:, :, offset : offset + row_count * col_count]
    column = jnp.arange(row_count * col_count) % col_count + col_step
    inside = (column >= 0) & (column < col_count)
    return jnp.where(inside, moved_cells, jnp.zeros_like(moved_cells))


def tap_patches(padded, depth_tap, row_tap, row_count, col_count):
    depth_len = padded.shape[1] - 2
    planes = padded[:, depth_tap : depth_tap + depth_len]
    stacked = jnp.stack(
        [shifted(planes, row_tap - 1, col_tap - 1, row_count, col_count) for col_tap in range(3)]
    )
    return stacked.reshape(3 * planes.shape[0], depth_len * planes.shape[2])


def conv_cube(padded, kernel, row_count, col_count):
    depth_len = padded.shape[1] - 2
    chans_in = kernel.shape[3]
    chans_out = kernel.shape[4]
    summed = jnp.zeros((chans_out, depth_len * padded.shape[2]), jnp.float32)
    for depth_tap in range(3):
        for row_tap in range(3):
            patches = tap_patches(padded, depth_tap, row_tap, row_count, col_count)
            tap_block = kernel[depth_tap, row_tap].reshape(3 * chans_in, chans_out)
            summed = summed + lax.dot_general(
                tap_block, patches, (((0,), (0,)), ((), ())), preferred_element_type=jnp.float32
            )
    return summed.reshape(chans_out, depth_len, padded.shape[2])


def weight_terms(padded, grad_out, row_count, col_count):
    chans_in = padded.shape[0]
    chans_out = grad_out.shape[0]
    flat_grad = grad_out.reshape(chans_out, -1)
    pieces = []
    for depth_tap in range(3):
        for row_tap in range(3):
            patches = tap_patches(padded, depth_tap, row_tap, row_count, col_count)
            pieces.append(
                lax.dot_general(
                    patches, flat_grad, (((1,), (1,)), ((), ())), preferred_element_type=jnp.float32
                )
            )
    return jnp.stack(pieces).reshape(3, 3, 3, chans_in, chans_out)


def flip_taps(kernel):
    return jnp.transpose(kernel[::-1, ::-1, ::-1], (0, 1, 2, 4, 3))


def pool_matrix(row_count, col_count):
    cells = jnp.arange(row_count * col_count)
    target = cells // col_count // 2 * (col_count // 2) + cells % col_count // 2
    return (target[:, None] == jnp.arange(row_count * col_count // 4)[None, :]).astype(jnp.float32)


def pool_cube(values, matrix):
    chans, depth_len, plane_len = values.shape
    paired = values.reshape(chans, depth_len // 2, 2, plane_len).sum(axis=2)
    return jnp.einsum("cdp,pq->cdq", paired, matrix, precision=lax.Precision.HIGHEST) * 0.125


def upsample_cube(values, matrix):
    spread = jnp.einsum("cdq,pq->cdp", values, matrix, precision=lax.Precision.HIGHEST)
    return jnp.repeat(spread, 2, axis=1)


def gelu_fwd(values):
    return jax.nn.gelu(values, approximate=True)


def gelu_back(pre_values, upstream):
    return jax.vjp(gelu_fwd, pre_values)[1](upstream)[0]


def extend(field, width):
    return extended(field, (("space", 1),), width)


def swap_add(parts, axis):
    me = lax.axis_index(axis)
    halves = parts.reshape(2, -1)
    own = lax.dynamic_index_in_dim(halves, me, 0, keepdims=False)
    other = lax.dynamic_index_in_dim(halves, 1 - me, 0, keepdims=False)
    return own + lax.ppermute(other, axis, [(0, 1), (1, 0)])


def swap_join(part, axis):
    me = lax.axis_index(axis)
    theirs = lax.ppermute(part, axis, [(0, 1), (1, 0)])
    first = jnp.where(me == 0, part, theirs)
    second = jnp.where(me == 0, theirs, part)
    return jnp.concatenate([first, second])


def mean_terms(terms, samples):
    axes = ("rows", "z_high", "space")
    devices = lax.axis_size("rows") * lax.axis_size("z_high") * lax.axis_size("space")
    flat = jnp.concatenate([term.reshape(-1) for term in terms])
    total = flat.shape[0]
    padded = -(-total // (4 * devices)) * 4 * devices
    own = swap_add(jnp.pad(flat, (0, padded - total)), "core")
    own = swap_add(own, "x_low")
    pieces = lax.all_to_all(own.reshape(devices, -1), axes, 0, 0, tiled=True)
    piece = (pieces.sum(axis=0) / samples).astype(jnp.bfloat16)
    spread = jnp.broadcast_to(piece, (devices,) + piece.shape)
    mine = lax.all_to_all(spread, axes, 0, 0, tiled=True).reshape(-1)
    gathered = swap_join(swap_join(mine, "x_low"), "core")[:total].astype(jnp.float32)
    results = []
    start = 0
    for term in terms:
        results.append(gathered[start : start + term.size].reshape(term.shape))
        start += term.size
    return tuple(results)


def shards(activations, cotangent, weight_mid, weight_deep):
    row_count = ROWS
    col_count = COLS
    source = activations[0]
    matrix = pool_matrix(row_count, col_count)
    source_ext = extend(source, 1)
    mid_pre = conv_cube(source_ext, weight_mid, row_count, col_count)
    pooled_ext = extend(pool_cube(gelu_fwd(mid_pre), matrix).astype(jnp.bfloat16), 1)
    deep_pre = conv_cube(pooled_ext, weight_deep, row_count // 2, col_count // 2)
    deep_grad = gelu_back(deep_pre, cotangent[0].astype(jnp.float32)).astype(jnp.bfloat16)
    deep_terms = weight_terms(pooled_ext, deep_grad, row_count // 2, col_count // 2)
    samples = 1
    for axis in SAMPLE_AXES:
        samples *= lax.axis_size(axis)
    back_pooled = conv_cube(
        extend(deep_grad, 1), flip_taps(weight_deep), row_count // 2, col_count // 2
    )
    spread = upsample_cube(back_pooled, matrix) * 0.125
    mid_grad = gelu_back(mid_pre, spread).astype(jnp.bfloat16)
    mid_terms = weight_terms(source_ext, mid_grad, row_count, col_count)
    grad_input = conv_cube(extend(mid_grad, 1), flip_taps(weight_mid), row_count, col_count).astype(
        jnp.bfloat16
    )
    grad_mid, grad_deep = mean_terms((mid_terms, deep_terms), samples)
    return (grad_input[None], grad_mid, grad_deep)


SAMPLE_AXES = ("rows", "x_low", "z_high", "core")


def solution(mesh):
    samples, slabs = mesh.devices.shape
    split = Mesh(mesh.devices.reshape(samples // 8, 2, 2, 2, slabs), SAMPLE_AXES + ("space",))
    in_specs = (P(SAMPLE_AXES, None, "space", None), P(SAMPLE_AXES, None, "space", None), P(), P())
    out_specs = (P(SAMPLE_AXES, None, "space", None), P(), P())
    return jax.shard_map(shards, mesh=split, in_specs=in_specs, out_specs=out_specs, check_vma=False)
```

profile of v0, /device:TPU:1, one launch (start us, length us, event | category | flops | bytes accessed | tf_op | source)
XLA Modules:
  0.0 189.2 jit_solution(13211840617532269973)
XLA Ops:
  1.6 1.3 collective-permute-start.1
  2.9 5.5 %collective-permute-start = (bf16[32,1,256]{2,1,0:T(2,128)(2,1)S(1)}, bf16[32,1,256]{2,1,0:T(2,128)(2,1)S(1)}, u32[]{:S(2)}, u32[]{:S(2)}) collective-permute-start(bf16[32,1,256]{2,1,0:T(2,128)(2,1)S(1)} %get-tuple-element.145), channel_id=1, source_target_pairs={{0,1},{1,2},{2,3},{3,4},{4,5},{6,7},{7,8},{8,9},{9,10},{10,11},{12... | collective-permute-start | bytes 49160 | tf_op jit(solution)/shard_map/ppermute | solution.py:15
  17.0 1.3 collective-permute-start.3
  18.3 4.6 %collective-permute-start.2 = (bf16[64,1,64]{2,0,1:T(8,128)(2,1)S(1)}, bf16[64,1,64]{2,0,1:T(8,128)(2,1)S(1)}, u32[]{:S(2)}, u32[]{:S(2)}) collective-permute-start(bf16[64,1,64]{2,0,1:T(8,128)(2,1)S(1)} %get-tuple-element.234), channel_id=1, source_target_pairs={{0,1},{1,2},{2,3},{3,4},{4,5},{6,7},{7,8},{8,9},{9,10},{10,11},{12... | collective-permute-start | bytes 24584 | tf_op jit(solution)/shard_map/ppermute | solution.py:15
  43.3 1.3 collective-permute-start.5
  44.6 4.8 %collective-permute-start.4 = (bf16[128,1,64]{0,2,1:T(8,128)(2,1)S(1)}, bf16[128,1,64]{0,2,1:T(8,128)(2,1)S(1)}, u32[]{:S(2)}, u32[]{:S(2)}) collective-permute-start(bf16[128,1,64]{0,2,1:T(8,128)(2,1)S(1)} %get-tuple-element.216), channel_id=1, source_target_pairs={{0,1},{1,2},{2,3},{3,4},{4,5},{6,7},{7,8},{8,9},{9,10},{10,11},{12... | collective-permute-start | bytes 49160 | tf_op jit(solution)/shard_map/ppermute | solution.py:15
  57.4 1.1 fusion.43
  61.5 1.3 collective-permute-start.7
  62.8 5.8 %collective-permute-start.6 = (bf16[64,1,256]{2,1,0:T(2,128)(2,1)S(1)}, bf16[64,1,256]{2,1,0:T(2,128)(2,1)S(1)}, u32[]{:S(2)}, u32[]{:S(2)}) collective-permute-start(bf16[64,1,256]{2,1,0:T(2,128)(2,1)S(1)} %get-tuple-element.101), channel_id=1, source_target_pairs={{0,1},{1,2},{2,3},{3,4},{4,5},{6,7},{7,8},{8,9},{9,10},{10,11},{12... | collective-permute-start | bytes 98312 | tf_op jit(solution)/shard_map/ppermute | solution.py:15
  70.4 10.4 %collective-permute-start.8 = (f32[138240]{0:T(1024)S(1)}, f32[138240]{0:T(1024)S(1)}, u32[]{:S(2)}, u32[]{:S(2)}) collective-permute-start(f32[138240]{0:T(1024)S(1)} %bitcast.700), channel_id=1, source_target_pairs={{0,6},{6,0},{1,7},{7,1},{2,8},{8,2},{3,9},{9,3},{4,10},{10,4},{5,1... | collective-permute-start | bytes 1658888 | tf_op jit(solution)/shard_map/ppermute | solution.py:111
  81.3 1.7 select_bitcast_fusion
  83.0 2.4 %fusion.63 = (bf16[1,64,4,256]{3,2,1,0:T(4,128)(2,1)S(1)}, bf16[1,64,4,256]{3,2,1,0:T(4,128)(2,1)S(1)}, bf16[1,64,4,256]{3,2,1,0:T(4,128)(2,1)S(1)}, bf16[1,64,4...) fusion(bf16[64,4,256]{2,1,0:T(4,128)(2,1)S(1)} %get-tuple-eleme, ...), kind=kLoop, calls=%fused_computation.223 | loop fusion | flops 1048576 | bytes 2360064 | tf_op jit(solution)/shard_map/stack | solution.py:36
  88.7 1.5 dynamic-slice_reduce_fusion
  90.2 1.9 %collective-permute-start.9 = (f32[69120]{0:T(1024)S(1)}, f32[69120]{0:T(1024)S(1)}, u32[]{:S(2)}, u32[]{:S(2)}) collective-permute-start(f32[69120]{0:T(1024)S(1)} %get-tuple-element.3), channel_id=1, source_target_pairs={{0,24},{24,0},{1,25},{25,1},{2,26},{26,2},{3,27},{27,3},{4,28},{28... | collective-permute-start | bytes 829448 | tf_op jit(solution)/shard_map/ppermute | solution.py:111
  94.6 5.8 %collective-permute-done.9 = f32[69120]{0:T(1024)S(1)} collective-permute-done((f32[69120]{0:T(1024)S(1)}, f32[69120]{0:T(1024)S(1)}, u32[]{:S(2)}, u32[]{:S(2)}) %collective-permute-start.9) | collective-permute-done | bytes 276512 | tf_op jit(solution)/shard_map/ppermute | solution.py:111
  100.4 1.3 all_to_all.10
  101.7 22.2 %all-to-all-start = ((f32[192,1,360]{2,1,0:T(1,128)}), f32[192,1,360]{2,1,0:T(1,128)S(1)}, u32[]{:S(2)}, u32[]{:S(2)}) async-start(f32[192,1,360]{2,1,0:T(1,128)} %all_to_all.10), calls=%async_computation | async-start | bytes 589824 | tf_op jit(solution)/shard_map/all_to_all | solution.py:130
  125.3 15.8 %all-to-all-done = f32[192,1,360]{2,1,0:T(1,128)S(1)} async-done(((f32[192,1,360]{2,1,0:T(1,128)}), f32[192,1,360]{2,1,0:T(1,128)S(1)}, u32[]{:S(2)}, u32[]{:S(2)}) %all-to-all-start) | async-done | bytes 276512 | tf_op jit(solution)/shard_map/all_to_all | solution.py:130
  142.0 1.6 reduce.6
  144.4 11.3 %all-to-all-start.1 = ((bf16[192,2,180]{2,1,0:T(2,128)(2,1)}), bf16[192,2,180]{2,1,0:T(2,128)(2,1)S(1)}, u32[]{:S(2)}, u32[]{:S(2)}) async-start(bf16[192,2,180]{2,1,0:T(2,128)(2,1)} %reshape.481), calls=%async_computation.1 | async-start | bytes 393216 | tf_op jit(solution)/shard_map/all_to_all | solution.py:133
  156.1 15.3 %all-to-all-done.1 = bf16[192,2,180]{2,1,0:T(2,128)(2,1)S(1)} async-done(((bf16[192,2,180]{2,1,0:T(2,128)(2,1)}), bf16[192,2,180]{2,1,0:T(2,128)(2,1)S(1)}, u32[]{:S(2)}, u32[]{:S(2)}) %all-to-all-start.1) | async-done | bytes 138272 | tf_op jit(solution)/shard_map/all_to_all | solution.py:133
  172.9 2.2 %collective-permute-start.10 = (bf16[69120]{0:T(1024)(128)(2,1)S(1)}, bf16[69120]{0:T(1024)(128)(2,1)S(1)}, u32[]{:S(2)}, u32[]{:S(2)}) collective-permute-start(bf16[69120]{0:T(1024)(128)(2,1)S(1)} %reshape.469), channel_id=1, source_target_pairs={{0,24},{24,0},{1,25},{25,1},{2,26},{26,2},{3,27},{27,3},{4,28},{28... | collective-permute-start | bytes 414728 | tf_op jit(solution)/shard_map/ppermute | solution.py:116
  175.4 3.4 %collective-permute-done.10 = bf16[69120]{0:T(1024)(128)(2,1)S(1)} collective-permute-done((bf16[69120]{0:T(1024)(128)(2,1)S(1)}, bf16[69120]{0:T(1024)(128)(2,1)S(1)}, u32[]{:S(2)}, u32[]{:S(2)}) %collective-permute-start.10) | collective-permute-done | bytes 138272 | tf_op jit(solution)/shard_map/ppermute | solution.py:116
  178.8 7.0 %collective-permute-start.11 = (bf16[138240]{0:T(1024)(128)(2,1)S(1)}, bf16[138240]{0:T(1024)(128)(2,1)S(1)}, u32[]{:S(2)}, u32[]{:S(2)}) collective-permute-start(bf16[138240]{0:T(1024)(128)(2,1)S(1)} %pad_maximum_fusion.11), channel_id=1, source_target_pairs={{0,6},{6,0},{1,7},{7,1},{2,8},{8,2},{3,9},{9,3},{4,10},{10,4},{5,1... | collective-permute-start | bytes 829448 | tf_op jit(solution)/shard_map/ppermute | solution.py:116
  (348 shorter events, 55.7 us)
Async XLA Ops:
  1.6 9.6 %collective-permute-start.1 = (bf16[32,1,256]{2,1,0:T(2,128)(2,1)S(1)}, bf16[32,1,256]{2,1,0:T(2,128)(2,1)S(1)}, u32[]{:S(2)}, u32[]{:S(2)}) collective-permute-start(bf16[32,1,256]{2,1,0:T(2,128)(2,1)S(1)} %get-tuple-element.144), channel_id=1, source_target_pairs={{1,0},{2,1},{3,2},{4,3},{5,4},{7,6},{8,7},{9,8},{10,9},{11,10},{13... | collective-permute-start | bytes 49160 | tf_op jit(solution)/shard_map/ppermute | solution.py:18
  2.9 8.3 %collective-permute-start = (bf16[32,1,256]{2,1,0:T(2,128)(2,1)S(1)}, bf16[32,1,256]{2,1,0:T(2,128)(2,1)S(1)}, u32[]{:S(2)}, u32[]{:S(2)}) collective-permute-start(bf16[32,1,256]{2,1,0:T(2,128)(2,1)S(1)} %get-tuple-element.145), channel_id=1, source_target_pairs={{0,1},{1,2},{2,3},{3,4},{4,5},{6,7},{7,8},{8,9},{9,10},{10,11},{12... | collective-permute-start | bytes 49160 | tf_op jit(solution)/shard_map/ppermute | solution.py:15
  8.5 28.8 %copy-start.45 = (pred[64]{0:T(512)(128)(4,1)}, pred[64]{0:T(512)(128)(4,1)S(1)}, u32[]{:S(2)}) copy-start(pred[64]{0:T(512)(128)(4,1)S(1)} %get-tuple-element.275) | copy-start | bytes 196
  8.5 28.8 %copy-start.51 = (pred[64]{0:T(512)(128)(4,1)}, pred[64]{0:T(512)(128)(4,1)S(1)}, u32[]{:S(2)}) copy-start(pred[64]{0:T(512)(128)(4,1)S(1)} %get-tuple-element.274) | copy-start | bytes 196
  17.0 19.4 %collective-permute-start.3 = (bf16[64,1,64]{2,0,1:T(8,128)(2,1)S(1)}, bf16[64,1,64]{2,0,1:T(8,128)(2,1)S(1)}, u32[]{:S(2)}, u32[]{:S(2)}) collective-permute-start(bf16[64,1,64]{2,0,1:T(8,128)(2,1)S(1)} %get-tuple-element.233), channel_id=1, source_target_pairs={{1,0},{2,1},{3,2},{4,3},{5,4},{7,6},{8,7},{9,8},{10,9},{11,10},{13... | collective-permute-start | bytes 24584 | tf_op jit(solution)/shard_map/ppermute | solution.py:18
  18.3 18.1 %collective-permute-start.2 = (bf16[64,1,64]{2,0,1:T(8,128)(2,1)S(1)}, bf16[64,1,64]{2,0,1:T(8,128)(2,1)S(1)}, u32[]{:S(2)}, u32[]{:S(2)}) collective-permute-start(bf16[64,1,64]{2,0,1:T(8,128)(2,1)S(1)} %get-tuple-element.234), channel_id=1, source_target_pairs={{0,1},{1,2},{2,3},{3,4},{4,5},{6,7},{7,8},{8,9},{9,10},{10,11},{12... | collective-permute-start | bytes 24584 | tf_op jit(solution)/shard_map/ppermute | solution.py:15
  23.0 14.4 %copy-start.53 = (pred[64]{0:T(512)(128)(4,1)}, pred[64]{0:T(512)(128)(4,1)S(1)}, u32[]{:S(2)}) copy-start(pred[64]{0:T(512)(128)(4,1)S(1)} %compare_and_fusion.4) | copy-start | bytes 196
  43.3 7.5 %collective-permute-start.5 = (bf16[128,1,64]{0,2,1:T(8,128)(2,1)S(1)}, bf16[128,1,64]{0,2,1:T(8,128)(2,1)S(1)}, u32[]{:S(2)}, u32[]{:S(2)}) collective-permute-start(bf16[128,1,64]{0,2,1:T(8,128)(2,1)S(1)} %get-tuple-element.215), channel_id=1, source_target_pairs={{1,0},{2,1},{3,2},{4,3},{5,4},{7,6},{8,7},{9,8},{10,9},{11,10},{13... | collective-permute-start | bytes 49160 | tf_op jit(solution)/shard_map/ppermute | solution.py:18
  44.6 6.2 %collective-permute-start.4 = (bf16[128,1,64]{0,2,1:T(8,128)(2,1)S(1)}, bf16[128,1,64]{0,2,1:T(8,128)(2,1)S(1)}, u32[]{:S(2)}, u32[]{:S(2)}) collective-permute-start(bf16[128,1,64]{0,2,1:T(8,128)(2,1)S(1)} %get-tuple-element.216), channel_id=1, source_target_pairs={{0,1},{1,2},{2,3},{3,4},{4,5},{6,7},{7,8},{8,9},{9,10},{10,11},{12... | collective-permute-start | bytes 49160 | tf_op jit(solution)/shard_map/ppermute | solution.py:15
  61.5 19.8 %collective-permute-start.7 = (bf16[64,1,256]{2,1,0:T(2,128)(2,1)S(1)}, bf16[64,1,256]{2,1,0:T(2,128)(2,1)S(1)}, u32[]{:S(2)}, u32[]{:S(2)}) collective-permute-start(bf16[64,1,256]{2,1,0:T(2,128)(2,1)S(1)} %get-tuple-element.100), channel_id=1, source_target_pairs={{1,0},{2,1},{3,2},{4,3},{5,4},{7,6},{8,7},{9,8},{10,9},{11,10},{13... | collective-permute-start | bytes 98312 | tf_op jit(solution)/shard_map/ppermute | solution.py:18
  62.8 18.5 %collective-permute-start.6 = (bf16[64,1,256]{2,1,0:T(2,128)(2,1)S(1)}, bf16[64,1,256]{2,1,0:T(2,128)(2,1)S(1)}, u32[]{:S(2)}, u32[]{:S(2)}) collective-permute-start(bf16[64,1,256]{2,1,0:T(2,128)(2,1)S(1)} %get-tuple-element.101), channel_id=1, source_target_pairs={{0,1},{1,2},{2,3},{3,4},{4,5},{6,7},{7,8},{8,9},{9,10},{10,11},{12... | collective-permute-start | bytes 98312 | tf_op jit(solution)/shard_map/ppermute | solution.py:15
  70.4 17.8 %collective-permute-start.8 = (f32[138240]{0:T(1024)S(1)}, f32[138240]{0:T(1024)S(1)}, u32[]{:S(2)}, u32[]{:S(2)}) collective-permute-start(f32[138240]{0:T(1024)S(1)} %bitcast.700), channel_id=1, source_target_pairs={{0,6},{6,0},{1,7},{7,1},{2,8},{8,2},{3,9},{9,3},{4,10},{10,4},{5,1... | collective-permute-start | bytes 1658888 | tf_op jit(solution)/shard_map/ppermute | solution.py:111
  90.2 10.2 %collective-permute-start.9 = (f32[69120]{0:T(1024)S(1)}, f32[69120]{0:T(1024)S(1)}, u32[]{:S(2)}, u32[]{:S(2)}) collective-permute-start(f32[69120]{0:T(1024)S(1)} %get-tuple-element.3), channel_id=1, source_target_pairs={{0,24},{24,0},{1,25},{25,1},{2,26},{26,2},{3,27},{27,3},{4,28},{28... | collective-permute-start | bytes 829448 | tf_op jit(solution)/shard_map/ppermute | solution.py:111
  94.5 29.4 %copy-start.9 = (bf16[1,64,4,256]{3,2,1,0:T(4,128)(2,1)S(1)}, bf16[1,64,4,256]{3,2,1,0:T(4,128)(2,1)}, u32[]{:S(2)}) copy-start(bf16[1,64,4,256]{3,2,1,0:T(4,128)(2,1)} %get-tuple-element.265) | copy-start | bytes 393220
  94.5 29.4 %copy-start.10 = (bf16[1,64,4,256]{3,2,1,0:T(4,128)(2,1)S(1)}, bf16[1,64,4,256]{3,2,1,0:T(4,128)(2,1)}, u32[]{:S(2)}) copy-start(bf16[1,64,4,256]{3,2,1,0:T(4,128)(2,1)} %get-tuple-element.268) | copy-start | bytes 393220
  94.5 29.4 %copy-start.11 = (bf16[1,64,4,256]{3,2,1,0:T(4,128)(2,1)S(1)}, bf16[1,64,4,256]{3,2,1,0:T(4,128)(2,1)}, u32[]{:S(2)}) copy-start(bf16[1,64,4,256]{3,2,1,0:T(4,128)(2,1)} %get-tuple-element.269) | copy-start | bytes 393220
  101.7 22.7 %copy-start.40 = (bf16[192,32]{0,1:T(8,128)(2,1)S(1)}, bf16[192,32]{0,1:T(8,128)(2,1)}, u32[]{:S(2)}) copy-start(bf16[192,32]{0,1:T(8,128)(2,1)} %reshape_squeeze.137) | copy-start | bytes 36868
  101.7 39.4 %all-to-all-start = ((f32[192,1,360]{2,1,0:T(1,128)}), f32[192,1,360]{2,1,0:T(1,128)S(1)}, u32[]{:S(2)}, u32[]{:S(2)}) async-start(f32[192,1,360]{2,1,0:T(1,128)} %all_to_all.10), calls=%async_computation | async-start | bytes 589824 | tf_op jit(solution)/shard_map/all_to_all | solution.py:130
  125.1 30.6 %copy-start.37 = (bf16[192,32]{0,1:T(8,128)(2,1)S(1)}, bf16[192,32]{0,1:T(8,128)(2,1)}, u32[]{:S(2)}) copy-start(bf16[192,32]{0,1:T(8,128)(2,1)} %reshape_squeeze.140) | copy-start | bytes 36868
  141.3 14.5 %copy-start.36 = (bf16[192,32]{0,1:T(8,128)(2,1)S(1)}, bf16[192,32]{0,1:T(8,128)(2,1)}, u32[]{:S(2)}) copy-start(bf16[192,32]{0,1:T(8,128)(2,1)} %reshape_squeeze.141) | copy-start | bytes 36868
  144.4 27.0 %all-to-all-start.1 = ((bf16[192,2,180]{2,1,0:T(2,128)(2,1)}), bf16[192,2,180]{2,1,0:T(2,128)(2,1)S(1)}, u32[]{:S(2)}, u32[]{:S(2)}) async-start(bf16[192,2,180]{2,1,0:T(2,128)(2,1)} %reshape.481), calls=%async_computation.1 | async-start | bytes 393216 | tf_op jit(solution)/shard_map/all_to_all | solution.py:133
  155.9 19.3 %copy-start.35 = (bf16[192,32]{0,1:T(8,128)(2,1)S(1)}, bf16[192,32]{0,1:T(8,128)(2,1)}, u32[]{:S(2)}) copy-start(bf16[192,32]{0,1:T(8,128)(2,1)} %reshape_squeeze.142) | copy-start | bytes 36868
  172.9 5.8 %collective-permute-start.10 = (bf16[69120]{0:T(1024)(128)(2,1)S(1)}, bf16[69120]{0:T(1024)(128)(2,1)S(1)}, u32[]{:S(2)}, u32[]{:S(2)}) collective-permute-start(bf16[69120]{0:T(1024)(128)(2,1)S(1)} %reshape.469), channel_id=1, source_target_pairs={{0,24},{24,0},{1,25},{25,1},{2,26},{26,2},{3,27},{27,3},{4,28},{28... | collective-permute-start | bytes 414728 | tf_op jit(solution)/shard_map/ppermute | solution.py:116
  178.8 8.3 %collective-permute-start.11 = (bf16[138240]{0:T(1024)(128)(2,1)S(1)}, bf16[138240]{0:T(1024)(128)(2,1)S(1)}, u32[]{:S(2)}, u32[]{:S(2)}) collective-permute-start(bf16[138240]{0:T(1024)(128)(2,1)S(1)} %pad_maximum_fusion.11), channel_id=1, source_target_pairs={{0,6},{6,0},{1,7},{7,1},{2,8},{8,2},{3,9},{9,3},{4,10},{10,4},{5,1... | collective-permute-start | bytes 829448 | tf_op jit(solution)/shard_map/ppermute | solution.py:116
  (47 other events, 206.3 us)
where the time goes:
time: 190 us; the launch traced here: 189 us
  starting transfers between devices  81 us (43%)
  waiting for transfers between devices  40.4 us (21%)
  local copies, waits for them, and re-layouts  34.9 us (18%)
  other arithmetic  19.3 us (10%)
  matrix products  11 us (6%)
  between operations  2.77 us (1%)
    all_to_all x1, starting transfers between devices, mean_terms(): pieces = lax.all_to_all(own.reshape(devices, -1), axes, 0, 0, tiled=True)  22.2 us
    ppermute x4, starting transfers between devices, extended(): lax.ppermute(lax.slice_in_dim(block, block.shape[dim] - width, None, axis...  20.7 us
    all_to_all x1, waiting for transfers between devices, mean_terms(): pieces = lax.all_to_all(own.reshape(devices, -1), axes, 0, 0, tiled=True)  15.8 us
    all_to_all x1, waiting for transfers between devices, mean_terms(): mine = lax.all_to_all(spread, axes, 0, 0, tiled=True).reshape(-1)  15.3 us
    another operation x44, other arithmetic, tap_patches(): jnp.stack([shifted(planes, row_tap - 1, col_tap - 1, row_count, col_count...  12.9 us
    ppermute x2, starting transfers between devices, swap_add(): return own + lax.ppermute(other, axis, [(0, 1), (1, 0)])  12.3 us
    all_to_all x1, starting transfers between devices, mean_terms(): mine = lax.all_to_all(spread, axes, 0, 0, tiled=True).reshape(-1)  11.3 us
    ppermute x2, starting transfers between devices, swap_join(): theirs = lax.ppermute(part, axis, [(0, 1), (1, 0)])  9.25 us
  transfers between devices with their start and end apart: 14, of which 4 were waited for; matrix products, arithmetic and copies ran while one was open for 16% of the time, Pallas kernels for 0%

commit v1 on v0

--- a/solution.py
+++ b/solution.py
@@ -120,18 +120,21 @@
 
 
 def mean_terms(terms, samples):
-    axes = ("rows", "z_high", "space")
-    devices = lax.axis_size("rows") * lax.axis_size("z_high") * lax.axis_size("space")
+    axes = ("y_high", "x_high", "z_high", "space")
+    devices = 1
+    for axis in axes:
+        devices *= lax.axis_size(axis)
     flat = jnp.concatenate([term.reshape(-1) for term in terms])
     total = flat.shape[0]
-    padded = -(-total // (4 * devices)) * 4 * devices
+    padded = -(-total // (8 * devices)) * 8 * devices
     own = swap_add(jnp.pad(flat, (0, padded - total)), "core")
     own = swap_add(own, "x_low")
+    own = swap_add(own, "y_low")
     pieces = lax.all_to_all(own.reshape(devices, -1), axes, 0, 0, tiled=True)
     piece = (pieces.sum(axis=0) / samples).astype(jnp.bfloat16)
     spread = jnp.broadcast_to(piece, (devices,) + piece.shape)
     mine = lax.all_to_all(spread, axes, 0, 0, tiled=True).reshape(-1)
-    gathered = swap_join(swap_join(mine, "x_low"), "core")[:total].astype(jnp.float32)
+    gathered = swap_join(swap_join(swap_join(mine, "y_low"), "x_low"), "core")[:total].astype(jnp.float32)
     results = []
     start = 0
     for term in terms:
@@ -167,12 +170,12 @@
     return (grad_input[None], grad_mid, grad_deep)
 
 
-SAMPLE_AXES = ("rows", "x_low", "z_high", "core")
+SAMPLE_AXES = ("y_high", "y_low", "x_high", "x_low", "z_high", "core")
 
 
 def solution(mesh):
     samples, slabs = mesh.devices.shape
-    split = Mesh(mesh.devices.reshape(samples // 8, 2, 2, 2, slabs), SAMPLE_AXES + ("space",))
+    split = Mesh(mesh.devices.reshape(samples // 32, 2, 2, 2, 2, 2, slabs), SAMPLE_AXES + ("space",))
     in_specs = (P(SAMPLE_AXES, None, "space", None), P(SAMPLE_AXES, None, "space", None), P(), P())
     out_specs = (P(SAMPLE_AXES, None, "space", None), P(), P())
     return jax.shard_map(shards, mesh=split, in_specs=in_specs, out_specs=out_specs, check_vma=False)

time: 190 us -> 194 us (1.021)
  waiting for transfers between devices: 40.4 us -> 47 us
    all_to_all x1, starting transfers between devices: 11.3 us -> 5.94 us  [mean_terms(): mine = lax.all_to_all(spread, axes, 0, 0, tiled=True).reshape(-1)]
    ppermute x2 -> x3, waiting for transfers between devices: 5.83 us -> 10.8 us  [swap_add(): return own + lax.ppermute(other, axis, [(0, 1), (1, 0)])]
    ppermute x2 -> x3, starting transfers between devices: 9.25 us -> 13.3 us  [swap_join(): theirs = lax.ppermute(part, axis, [(0, 1), (1, 0)])]
    ppermute x2 -> x3, waiting for transfers between devices: 3.38 us -> 5.72 us  [swap_join(): theirs = lax.ppermute(part, axis, [(0, 1), (1, 0)])]
    ppermute x2 -> x3, starting transfers between devices: 12.3 us -> 14.2 us  [swap_add(): return own + lax.ppermute(other, axis, [(0, 1), (1, 0)])]
    unnamed x134 -> x126, local copies, waits for them, and re-layouts: 4.23 us -> 2.96 us
  transfers between devices with their start and end apart: 14 -> 16, of which waited for: 4 -> 6; matrix products, arithmetic and copies ran while one was open for 16% -> 15% of each run, Pallas kernels for 0% -> 0%
where the time goes in v1:
time: 194 us; the launch traced here: 193 us
  starting transfers between devices  79.6 us (41%)
  waiting for transfers between devices  47 us (24%)
  local copies, waits for them, and re-layouts  34 us (18%)
  other arithmetic  18.2 us (9%)
  matrix products  11 us (6%)
  between operations  2.77 us (1%)
    ppermute x4, starting transfers between devices, extended(): lax.ppermute(lax.slice_in_dim(block, block.shape[dim] - width, None, axis...  20.7 us
    all_to_all x1, starting transfers between devices, mean_terms(): pieces = lax.all_to_all(own.reshape(devices, -1), axes, 0, 0, tiled=True)  20.3 us
    all_to_all x1, waiting for transfers between devices, mean_terms(): mine = lax.all_to_all(spread, axes, 0, 0, tiled=True).reshape(-1)  15.4 us
    all_to_all x1, waiting for transfers between devices, mean_terms(): pieces = lax.all_to_all(own.reshape(devices, -1), axes, 0, 0, tiled=True)  15.1 us
    ppermute x3, starting transfers between devices, swap_add(): return own + lax.ppermute(other, axis, [(0, 1), (1, 0)])  14.2 us
    ppermute x3, starting transfers between devices, swap_join(): theirs = lax.ppermute(part, axis, [(0, 1), (1, 0)])  13.3 us
    another operation x44, other arithmetic, tap_patches(): jnp.stack([shifted(planes, row_tap - 1, col_tap - 1, row_count, col_count...  12.8 us
    ppermute x3, waiting for transfers between devices, swap_add(): return own + lax.ppermute(other, axis, [(0, 1), (1, 0)])  10.8 us
  transfers between devices with their start and end apart: 16, of which 6 were waited for; matrix products, arithmetic and copies ran while one was open for 15% of the time, Pallas kernels for 0%

profile of v1, /device:TPU:1, one launch (start us, length us, event | category | flops | bytes accessed | tf_op | source)
XLA Modules:
  0.0 192.6 jit_solution(1560021052166691960)
XLA Ops:
  1.6 1.3 collective-permute-start.1
  2.9 5.5 %collective-permute-start = (bf16[32,1,256]{2,1,0:T(2,128)(2,1)S(1)}, bf16[32,1,256]{2,1,0:T(2,128)(2,1)S(1)}, u32[]{:S(2)}, u32[]{:S(2)}) collective-permute-start(bf16[32,1,256]{2,1,0:T(2,128)(2,1)S(1)} %get-tuple-element.149), channel_id=1, source_target_pairs={{0,1},{1,2},{2,3},{3,4},{4,5},{6,7},{7,8},{8,9},{9,10},{10,11},{12... | collective-permute-start | bytes 49160 | tf_op jit(solution)/shard_map/ppermute | solution.py:15
  17.0 1.3 collective-permute-start.3
  18.3 4.6 %collective-permute-start.2 = (bf16[64,1,64]{2,0,1:T(8,128)(2,1)S(1)}, bf16[64,1,64]{2,0,1:T(8,128)(2,1)S(1)}, u32[]{:S(2)}, u32[]{:S(2)}) collective-permute-start(bf16[64,1,64]{2,0,1:T(8,128)(2,1)S(1)} %get-tuple-element.238), channel_id=1, source_target_pairs={{0,1},{1,2},{2,3},{3,4},{4,5},{6,7},{7,8},{8,9},{9,10},{10,11},{12... | collective-permute-start | bytes 24584 | tf_op jit(solution)/shard_map/ppermute | solution.py:15
  43.3 1.3 collective-permute-start.5
  44.6 4.8 %collective-permute-start.4 = (bf16[128,1,64]{0,2,1:T(8,128)(2,1)S(1)}, bf16[128,1,64]{0,2,1:T(8,128)(2,1)S(1)}, u32[]{:S(2)}, u32[]{:S(2)}) collective-permute-start(bf16[128,1,64]{0,2,1:T(8,128)(2,1)S(1)} %get-tuple-element.220), channel_id=1, source_target_pairs={{0,1},{1,2},{2,3},{3,4},{4,5},{6,7},{7,8},{8,9},{9,10},{10,11},{12... | collective-permute-start | bytes 49160 | tf_op jit(solution)/shard_map/ppermute | solution.py:15
  62.7 5.8 %collective-permute-start.6 = (bf16[64,1,256]{2,1,0:T(2,128)(2,1)S(1)}, bf16[64,1,256]{2,1,0:T(2,128)(2,1)S(1)}, u32[]{:S(2)}, u32[]{:S(2)}) collective-permute-start(bf16[64,1,256]{2,1,0:T(2,128)(2,1)S(1)} %get-tuple-element.105), channel_id=1, source_target_pairs={{0,1},{1,2},{2,3},{3,4},{4,5},{6,7},{7,8},{8,9},{9,10},{10,11},{12... | collective-permute-start | bytes 98312 | tf_op jit(solution)/shard_map/ppermute | solution.py:15
  70.4 10.4 %collective-permute-start.8 = (f32[138240]{0:T(1024)S(1)}, f32[138240]{0:T(1024)S(1)}, u32[]{:S(2)}, u32[]{:S(2)}) collective-permute-start(f32[138240]{0:T(1024)S(1)} %bitcast.700), channel_id=1, source_target_pairs={{0,6},{6,0},{1,7},{7,1},{2,8},{8,2},{3,9},{9,3},{4,10},{10,4},{5,1... | collective-permute-start | bytes 1658888 | tf_op jit(solution)/shard_map/ppermute | solution.py:111
  81.2 1.7 select_bitcast_fusion
  82.9 2.3 %fusion.63 = (bf16[1,64,4,256]{3,2,1,0:T(4,128)(2,1)S(1)}, bf16[1,64,4,256]{3,2,1,0:T(4,128)(2,1)S(1)}, bf16[1,64,4,256]{3,2,1,0:T(4,128)(2,1)S(1)}, bf16[1,64,4...) fusion(bf16[64,4,256]{2,1,0:T(4,128)(2,1)S(1)} %get-tuple-eleme, ...), kind=kLoop, calls=%fused_computation.226 | loop fusion | flops 1048576 | bytes 2360064 | tf_op jit(solution)/shard_map/stack | solution.py:36
  88.8 1.5 dynamic-slice_reduce_fusion
  90.3 1.9 collective-permute-start.9
  93.8 6.7 %collective-permute-done.9 = f32[69120]{0:T(1024)S(1)} collective-permute-done((f32[69120]{0:T(1024)S(1)}, f32[69120]{0:T(1024)S(1)}, u32[]{:S(2)}, u32[]{:S(2)}) %collective-permute-start.9) | collective-permute-done | bytes 276512 | tf_op jit(solution)/shard_map/ppermute | solution.py:111
  101.5 1.9 collective-permute-start.10
  103.6 4.2 %collective-permute-done.10 = f32[34560]{0:T(1024)S(1)} collective-permute-done((f32[34560]{0:T(1024)S(1)}, f32[34560]{0:T(1024)S(1)}, u32[]{:S(2)}, u32[]{:S(2)}) %collective-permute-start.10) | collective-permute-done | bytes 138272 | tf_op jit(solution)/shard_map/ppermute | solution.py:111
  108.7 20.3 %all-to-all-start = ((f32[96,1,360]{2,1,0:T(1,128)}), f32[96,1,360]{2,1,0:T(1,128)S(1)}, u32[]{:S(2)}, u32[]{:S(2)}) async-start(f32[96,1,360]{2,1,0:T(1,128)} %all_to_all.10), calls=%async_computation | async-start | bytes 294912 | tf_op jit(solution)/shard_map/all_to_all | solution.py:133
  129.4 15.1 %all-to-all-done = f32[96,1,360]{2,1,0:T(1,128)S(1)} async-done(((f32[96,1,360]{2,1,0:T(1,128)}), f32[96,1,360]{2,1,0:T(1,128)S(1)}, u32[]{:S(2)}, u32[]{:S(2)}) %all-to-all-start) | async-done | bytes 138272 | tf_op jit(solution)/shard_map/all_to_all | solution.py:133
  147.1 5.9 %all-to-all-start.1 = ((bf16[96,2,180]{2,1,0:T(2,128)(2,1)}), bf16[96,2,180]{2,1,0:T(2,128)(2,1)S(1)}, u32[]{:S(2)}, u32[]{:S(2)}) async-start(bf16[96,2,180]{2,1,0:T(2,128)(2,1)} %reshape.487), calls=%async_computation.1 | async-start | bytes 196608 | tf_op jit(solution)/shard_map/all_to_all | solution.py:136
  153.2 15.4 %all-to-all-done.1 = bf16[96,2,180]{2,1,0:T(2,128)(2,1)S(1)} async-done(((bf16[96,2,180]{2,1,0:T(2,128)(2,1)}), bf16[96,2,180]{2,1,0:T(2,128)(2,1)S(1)}, u32[]{:S(2)}, u32[]{:S(2)}) %all-to-all-start.1) | async-done | bytes 69152 | tf_op jit(solution)/shard_map/all_to_all | solution.py:136
  169.4 2.3 %collective-permute-start.11 = (bf16[34560]{0:T(1024)(128)(2,1)S(1)}, bf16[34560]{0:T(1024)(128)(2,1)S(1)}, u32[]{:S(2)}, u32[]{:S(2)}) collective-permute-start(bf16[34560]{0:T(1024)(128)(2,1)S(1)} %reshape.473), channel_id=1, source_target_pairs={{0,96},{96,0},{1,97},{97,1},{2,98},{98,2},{3,99},{99,3},{4,100},{1... | collective-permute-start | bytes 207368 | tf_op jit(solution)/shard_map/ppermute | solution.py:116
  172.1 2.3 %collective-permute-done.11 = bf16[34560]{0:T(1024)(128)(2,1)S(1)} collective-permute-done((bf16[34560]{0:T(1024)(128)(2,1)S(1)}, bf16[34560]{0:T(1024)(128)(2,1)S(1)}, u32[]{:S(2)}, u32[]{:S(2)}) %collective-permute-start.11) | collective-permute-done | bytes 69152 | tf_op jit(solution)/shard_map/ppermute | solution.py:116
  174.5 2.2 %collective-permute-start.12 = (bf16[69120]{0:T(1024)(128)(2,1)S(1)}, bf16[69120]{0:T(1024)(128)(2,1)S(1)}, u32[]{:S(2)}, u32[]{:S(2)}) collective-permute-start(bf16[69120]{0:T(1024)(128)(2,1)S(1)} %pad_maximum_fusion.21), channel_id=1, source_target_pairs={{0,24},{24,0},{1,25},{25,1},{2,26},{26,2},{3,27},{27,3},{4,28},{28... | collective-permute-start | bytes 414728 | tf_op jit(solution)/shard_map/ppermute | solution.py:116
  176.9 3.4 %collective-permute-done.12 = bf16[69120]{0:T(1024)(128)(2,1)S(1)} collective-permute-done((bf16[69120]{0:T(1024)(128)(2,1)S(1)}, bf16[69120]{0:T(1024)(128)(2,1)S(1)}, u32[]{:S(2)}, u32[]{:S(2)}) %collective-permute-start.12) | collective-permute-done | bytes 138272 | tf_op jit(solution)/shard_map/ppermute | solution.py:116
  180.4 8.8 %collective-permute-start.13 = (bf16[138240]{0:T(1024)(128)(2,1)S(1)}, bf16[138240]{0:T(1024)(128)(2,1)S(1)}, u32[]{:S(2)}, u32[]{:S(2)}) collective-permute-start(bf16[138240]{0:T(1024)(128)(2,1)S(1)} %pad_maximum_fusion.11), channel_id=1, source_target_pairs={{0,6},{6,0},{1,7},{7,1},{2,8},{8,2},{3,9},{9,3},{4,10},{10,4},{5,1... | collective-permute-start | bytes 829448 | tf_op jit(solution)/shard_map/ppermute | solution.py:116
  (349 shorter events, 59.0 us)
Async XLA Ops:
  1.6 9.6 %collective-permute-start.1 = (bf16[32,1,256]{2,1,0:T(2,128)(2,1)S(1)}, bf16[32,1,256]{2,1,0:T(2,128)(2,1)S(1)}, u32[]{:S(2)}, u32[]{:S(2)}) collective-permute-start(bf16[32,1,256]{2,1,0:T(2,128)(2,1)S(1)} %get-tuple-element.148), channel_id=1, source_target_pairs={{1,0},{2,1},{3,2},{4,3},{5,4},{7,6},{8,7},{9,8},{10,9},{11,10},{13... | collective-permute-start | bytes 49160 | tf_op jit(solution)/shard_map/ppermute | solution.py:18
  2.9 8.3 %collective-permute-start = (bf16[32,1,256]{2,1,0:T(2,128)(2,1)S(1)}, bf16[32,1,256]{2,1,0:T(2,128)(2,1)S(1)}, u32[]{:S(2)}, u32[]{:S(2)}) collective-permute-start(bf16[32,1,256]{2,1,0:T(2,128)(2,1)S(1)} %get-tuple-element.149), channel_id=1, source_target_pairs={{0,1},{1,2},{2,3},{3,4},{4,5},{6,7},{7,8},{8,9},{9,10},{10,11},{12... | collective-permute-start | bytes 49160 | tf_op jit(solution)/shard_map/ppermute | solution.py:15
  8.5 28.8 %copy-start.41 = (pred[64]{0:T(512)(128)(4,1)}, pred[64]{0:T(512)(128)(4,1)S(1)}, u32[]{:S(2)}) copy-start(pred[64]{0:T(512)(128)(4,1)S(1)} %get-tuple-element.279) | copy-start | bytes 196
  8.5 28.8 %copy-start.47 = (pred[64]{0:T(512)(128)(4,1)}, pred[64]{0:T(512)(128)(4,1)S(1)}, u32[]{:S(2)}) copy-start(pred[64]{0:T(512)(128)(4,1)S(1)} %get-tuple-element.278) | copy-start | bytes 196
  17.0 19.3 %collective-permute-start.3 = (bf16[64,1,64]{2,0,1:T(8,128)(2,1)S(1)}, bf16[64,1,64]{2,0,1:T(8,128)(2,1)S(1)}, u32[]{:S(2)}, u32[]{:S(2)}) collective-permute-start(bf16[64,1,64]{2,0,1:T(8,128)(2,1)S(1)} %get-tuple-element.237), channel_id=1, source_target_pairs={{1,0},{2,1},{3,2},{4,3},{5,4},{7,6},{8,7},{9,8},{10,9},{11,10},{13... | collective-permute-start | bytes 24584 | tf_op jit(solution)/shard_map/ppermute | solution.py:18
  18.3 18.0 %collective-permute-start.2 = (bf16[64,1,64]{2,0,1:T(8,128)(2,1)S(1)}, bf16[64,1,64]{2,0,1:T(8,128)(2,1)S(1)}, u32[]{:S(2)}, u32[]{:S(2)}) collective-permute-start(bf16[64,1,64]{2,0,1:T(8,128)(2,1)S(1)} %get-tuple-element.238), channel_id=1, source_target_pairs={{0,1},{1,2},{2,3},{3,4},{4,5},{6,7},{7,8},{8,9},{9,10},{10,11},{12... | collective-permute-start | bytes 24584 | tf_op jit(solution)/shard_map/ppermute | solution.py:15
  43.3 7.5 %collective-permute-start.5 = (bf16[128,1,64]{0,2,1:T(8,128)(2,1)S(1)}, bf16[128,1,64]{0,2,1:T(8,128)(2,1)S(1)}, u32[]{:S(2)}, u32[]{:S(2)}) collective-permute-start(bf16[128,1,64]{0,2,1:T(8,128)(2,1)S(1)} %get-tuple-element.219), channel_id=1, source_target_pairs={{1,0},{2,1},{3,2},{4,3},{5,4},{7,6},{8,7},{9,8},{10,9},{11,10},{13... | collective-permute-start | bytes 49160 | tf_op jit(solution)/shard_map/ppermute | solution.py:18
  44.6 6.2 %collective-permute-start.4 = (bf16[128,1,64]{0,2,1:T(8,128)(2,1)S(1)}, bf16[128,1,64]{0,2,1:T(8,128)(2,1)S(1)}, u32[]{:S(2)}, u32[]{:S(2)}) collective-permute-start(bf16[128,1,64]{0,2,1:T(8,128)(2,1)S(1)} %get-tuple-element.220), channel_id=1, source_target_pairs={{0,1},{1,2},{2,3},{3,4},{4,5},{6,7},{7,8},{8,9},{9,10},{10,11},{12... | collective-permute-start | bytes 49160 | tf_op jit(solution)/shard_map/ppermute | solution.py:15
  61.4 19.8 %collective-permute-start.7 = (bf16[64,1,256]{2,1,0:T(2,128)(2,1)S(1)}, bf16[64,1,256]{2,1,0:T(2,128)(2,1)S(1)}, u32[]{:S(2)}, u32[]{:S(2)}) collective-permute-start(bf16[64,1,256]{2,1,0:T(2,128)(2,1)S(1)} %get-tuple-element.104), channel_id=1, source_target_pairs={{1,0},{2,1},{3,2},{4,3},{5,4},{7,6},{8,7},{9,8},{10,9},{11,10},{13... | collective-permute-start | bytes 98312 | tf_op jit(solution)/shard_map/ppermute | solution.py:18
  62.7 18.5 %collective-permute-start.6 = (bf16[64,1,256]{2,1,0:T(2,128)(2,1)S(1)}, bf16[64,1,256]{2,1,0:T(2,128)(2,1)S(1)}, u32[]{:S(2)}, u32[]{:S(2)}) collective-permute-start(bf16[64,1,256]{2,1,0:T(2,128)(2,1)S(1)} %get-tuple-element.105), channel_id=1, source_target_pairs={{0,1},{1,2},{2,3},{3,4},{4,5},{6,7},{7,8},{8,9},{9,10},{10,11},{12... | collective-permute-start | bytes 98312 | tf_op jit(solution)/shard_map/ppermute | solution.py:15
  70.4 18.0 %collective-permute-start.8 = (f32[138240]{0:T(1024)S(1)}, f32[138240]{0:T(1024)S(1)}, u32[]{:S(2)}, u32[]{:S(2)}) collective-permute-start(f32[138240]{0:T(1024)S(1)} %bitcast.700), channel_id=1, source_target_pairs={{0,6},{6,0},{1,7},{7,1},{2,8},{8,2},{3,9},{9,3},{4,10},{10,4},{5,1... | collective-permute-start | bytes 1658888 | tf_op jit(solution)/shard_map/ppermute | solution.py:111
  90.3 10.2 %collective-permute-start.9 = (f32[69120]{0:T(1024)S(1)}, f32[69120]{0:T(1024)S(1)}, u32[]{:S(2)}, u32[]{:S(2)}) collective-permute-start(f32[69120]{0:T(1024)S(1)} %get-tuple-element.3), channel_id=1, source_target_pairs={{0,24},{24,0},{1,25},{25,1},{2,26},{26,2},{3,27},{27,3},{4,28},{28... | collective-permute-start | bytes 829448 | tf_op jit(solution)/shard_map/ppermute | solution.py:111
  100.7 28.3 %copy-start.34 = (bf16[192,32]{0,1:T(8,128)(2,1)S(1)}, bf16[192,32]{0,1:T(8,128)(2,1)}, u32[]{:S(2)}) copy-start(bf16[192,32]{0,1:T(8,128)(2,1)} %reshape_squeeze.139) | copy-start | bytes 36868
  101.5 6.3 %collective-permute-start.10 = (f32[34560]{0:T(1024)S(1)}, f32[34560]{0:T(1024)S(1)}, u32[]{:S(2)}, u32[]{:S(2)}) collective-permute-start(f32[34560]{0:T(1024)S(1)} %get-tuple-element.5), channel_id=1, source_target_pairs={{0,96},{96,0},{1,97},{97,1},{2,98},{98,2},{3,99},{99,3},{4,100},{1... | collective-permute-start | bytes 414728 | tf_op jit(solution)/shard_map/ppermute | solution.py:111
  103.4 25.8 %copy-start.33 = (bf16[192,32]{0,1:T(8,128)(2,1)S(1)}, bf16[192,32]{0,1:T(8,128)(2,1)}, u32[]{:S(2)}) copy-start(bf16[192,32]{0,1:T(8,128)(2,1)} %reshape_squeeze.140) | copy-start | bytes 36868
  108.7 35.8 %all-to-all-start = ((f32[96,1,360]{2,1,0:T(1,128)}), f32[96,1,360]{2,1,0:T(1,128)S(1)}, u32[]{:S(2)}, u32[]{:S(2)}) async-start(f32[96,1,360]{2,1,0:T(1,128)} %all_to_all.10), calls=%async_computation | async-start | bytes 294912 | tf_op jit(solution)/shard_map/all_to_all | solution.py:133
  129.0 24.0 %copy-start.32 = (bf16[192,32]{0,1:T(8,128)(2,1)S(1)}, bf16[192,32]{0,1:T(8,128)(2,1)}, u32[]{:S(2)}) copy-start(bf16[192,32]{0,1:T(8,128)(2,1)} %reshape_squeeze.141) | copy-start | bytes 36868
  129.4 42.3 %copy-start.5 = (bf16[1,64,4,256]{3,2,1,0:T(4,128)(2,1)S(1)}, bf16[1,64,4,256]{3,2,1,0:T(4,128)(2,1)}, u32[]{:S(2)}) copy-start(bf16[1,64,4,256]{3,2,1,0:T(4,128)(2,1)} %get-tuple-element.270) | copy-start | bytes 393220
  129.4 42.3 %copy-start.6 = (bf16[1,64,4,256]{3,2,1,0:T(4,128)(2,1)S(1)}, bf16[1,64,4,256]{3,2,1,0:T(4,128)(2,1)}, u32[]{:S(2)}) copy-start(bf16[1,64,4,256]{3,2,1,0:T(4,128)(2,1)} %get-tuple-element.274) | copy-start | bytes 393220
  129.4 42.3 %copy-start.11 = (bf16[1,64,4,256]{3,2,1,0:T(4,128)(2,1)S(1)}, bf16[1,64,4,256]{3,2,1,0:T(4,128)(2,1)}, u32[]{:S(2)}) copy-start(bf16[1,64,4,256]{3,2,1,0:T(4,128)(2,1)} %get-tuple-element.7) | copy-start | bytes 393220
  147.1 21.5 %all-to-all-start.1 = ((bf16[96,2,180]{2,1,0:T(2,128)(2,1)}), bf16[96,2,180]{2,1,0:T(2,128)(2,1)S(1)}, u32[]{:S(2)}, u32[]{:S(2)}) async-start(bf16[96,2,180]{2,1,0:T(2,128)(2,1)} %reshape.487), calls=%async_computation.1 | async-start | bytes 196608 | tf_op jit(solution)/shard_map/all_to_all | solution.py:136
  169.4 5.1 %collective-permute-start.11 = (bf16[34560]{0:T(1024)(128)(2,1)S(1)}, bf16[34560]{0:T(1024)(128)(2,1)S(1)}, u32[]{:S(2)}, u32[]{:S(2)}) collective-permute-start(bf16[34560]{0:T(1024)(128)(2,1)S(1)} %reshape.473), channel_id=1, source_target_pairs={{0,96},{96,0},{1,97},{97,1},{2,98},{98,2},{3,99},{99,3},{4,100},{1... | collective-permute-start | bytes 207368 | tf_op jit(solution)/shard_map/ppermute | solution.py:116
  174.5 5.8 %collective-permute-start.12 = (bf16[69120]{0:T(1024)(128)(2,1)S(1)}, bf16[69120]{0:T(1024)(128)(2,1)S(1)}, u32[]{:S(2)}, u32[]{:S(2)}) collective-permute-start(bf16[69120]{0:T(1024)(128)(2,1)S(1)} %pad_maximum_fusion.21), channel_id=1, source_target_pairs={{0,24},{24,0},{1,25},{25,1},{2,26},{26,2},{3,27},{27,3},{4,28},{28... | collective-permute-start | bytes 414728 | tf_op jit(solution)/shard_map/ppermute | solution.py:116
  180.4 10.0 %collective-permute-start.13 = (bf16[138240]{0:T(1024)(128)(2,1)S(1)}, bf16[138240]{0:T(1024)(128)(2,1)S(1)}, u32[]{:S(2)}, u32[]{:S(2)}) collective-permute-start(bf16[138240]{0:T(1024)(128)(2,1)S(1)} %pad_maximum_fusion.11), channel_id=1, source_target_pairs={{0,6},{6,0},{1,7},{7,1},{2,8},{8,2},{3,9},{9,3},{4,10},{10,4},{5,1... | collective-permute-start | bytes 829448 | tf_op jit(solution)/shard_map/ppermute | solution.py:116
  (45 other events, 197.4 us)

commit v2 on v0

--- a/solution.py
+++ b/solution.py
@@ -119,7 +119,7 @@
     return jnp.concatenate([first, second])
 
 
-def mean_terms(terms, samples):
+def mean_terms(terms, samples, rider):
     axes = ("rows", "z_high", "space")
     devices = lax.axis_size("rows") * lax.axis_size("z_high") * lax.axis_size("space")
     flat = jnp.concatenate([term.reshape(-1) for term in terms])
@@ -127,6 +127,7 @@
     padded = -(-total // (4 * devices)) * 4 * devices
     own = swap_add(jnp.pad(flat, (0, padded - total)), "core")
     own = swap_add(own, "x_low")
+    own, rider = lax.optimization_barrier((own, rider))
     pieces = lax.all_to_all(own.reshape(devices, -1), axes, 0, 0, tiled=True)
     piece = (pieces.sum(axis=0) / samples).astype(jnp.bfloat16)
     spread = jnp.broadcast_to(piece, (devices,) + piece.shape)
@@ -137,7 +138,7 @@
     for term in terms:
         results.append(gathered[start : start + term.size].reshape(term.shape))
         start += term.size
-    return tuple(results)
+    return tuple(results), rider
 
 
 def shards(activations, cotangent, weight_mid, weight_deep):
@@ -160,10 +161,10 @@
     spread = upsample_cube(back_pooled, matrix) * 0.125
     mid_grad = gelu_back(mid_pre, spread).astype(jnp.bfloat16)
     mid_terms = weight_terms(source_ext, mid_grad, row_count, col_count)
+    (grad_mid, grad_deep), mid_grad = mean_terms((mid_terms, deep_terms), samples, mid_grad)
     grad_input = conv_cube(extend(mid_grad, 1), flip_taps(weight_mid), row_count, col_count).astype(
         jnp.bfloat16
     )
-    grad_mid, grad_deep = mean_terms((mid_terms, deep_terms), samples)
     return (grad_input[None], grad_mid, grad_deep)
 
 

time: 190 us -> 171 us (0.900)
  local copies, waits for them, and re-layouts: 34.9 us -> 21.4 us
  waiting for transfers between devices: 40.4 us -> 37.7 us
  other arithmetic: 19.3 us -> 16.9 us
    all_to_all x1, waiting for transfers between devices: 15.8 us -> 10 us  [mean_terms(): pieces = lax.all_to_all(own.reshape(devices, -1), axes, 0, 0, tiled=True)]
    another operation x9, local copies, waits for them, and re-layouts: 6.21 us -> 0.86 us  [conv_cube(): tap_block = kernel[depth_tap, row_tap].reshape(3 * chans_in, chans_out)]
    ppermute x2, waiting for transfers between devices: 5.83 us -> 8.61 us  [swap_add(): return own + lax.ppermute(other, axis, [(0, 1), (1, 0)])]
    unnamed x134 -> x76, local copies, waits for them, and re-layouts: 4.23 us -> 1.88 us
    mul x4 -> x3, local copies, waits for them, and re-layouts: 2.9 us -> 0.54 us  [shards(): spread = upsample_cube(back_pooled, matrix) * 0.125]
  transfers between devices with their start and end apart: 14 -> 14, of which waited for: 4 -> 6; matrix products, arithmetic and copies ran while one was open for 16% -> 9% of each run, Pallas kernels for 0% -> 0%
where the time goes in v2:
time: 171 us; the launch traced here: 170 us
  starting transfers between devices  81.6 us (48%)
  waiting for transfers between devices  37.7 us (22%)
  local copies, waits for them, and re-layouts  21.4 us (13%)
  other arithmetic  16.9 us (10%)
  matrix products  10.4 us (6%)
  between operations  2.43 us (1%)
    all_to_all x1, starting transfers between devices, mean_terms(): pieces = lax.all_to_all(own.reshape(devices, -1), axes, 0, 0, tiled=True)  21.8 us
    ppermute x4, starting transfers between devices, extended(): lax.ppermute(lax.slice_in_dim(block, block.shape[dim] - width, None, axis...  19.4 us
    all_to_all x1, waiting for transfers between devices, mean_terms(): mine = lax.all_to_all(spread, axes, 0, 0, tiled=True).reshape(-1)  15.1 us
    ppermute x2, starting transfers between devices, swap_add(): return own + lax.ppermute(other, axis, [(0, 1), (1, 0)])  13.8 us
    another operation x44, other arithmetic, tap_patches(): jnp.stack([shifted(planes, row_tap - 1, col_tap - 1, row_count, col_count...  11.9 us
    all_to_all x1, starting transfers between devices, mean_terms(): mine = lax.all_to_all(spread, axes, 0, 0, tiled=True).reshape(-1)  11.9 us
    all_to_all x1, waiting for transfers between devices, mean_terms(): pieces = lax.all_to_all(own.reshape(devices, -1), axes, 0, 0, tiled=True)  10 us
    ppermute x2, starting transfers between devices, swap_join(): theirs = lax.ppermute(part, axis, [(0, 1), (1, 0)])  9.38 us
  transfers between devices with their start and end apart: 14, of which 6 were waited for; matrix products, arithmetic and copies ran while one was open for 9% of the time, Pallas kernels for 0%

profile of v2, /device:TPU:1, one launch (start us, length us, event | category | flops | bytes accessed | tf_op | source)
XLA Modules:
  0.0 170.4 jit_solution(614287930751660528)
XLA Ops:
  1.7 1.3 collective-permute-start.1
  3.0 5.5 %collective-permute-start = (bf16[32,1,256]{2,1,0:T(2,128)(2,1)S(1)}, bf16[32,1,256]{2,1,0:T(2,128)(2,1)S(1)}, u32[]{:S(2)}, u32[]{:S(2)}) collective-permute-start(bf16[32,1,256]{2,1,0:T(2,128)(2,1)S(1)} %get-tuple-element.150), channel_id=1, source_target_pairs={{0,1},{1,2},{2,3},{3,4},{4,5},{6,7},{7,8},{8,9},{9,10},{10,11},{12... | collective-permute-start | bytes 49160 | tf_op jit(solution)/shard_map/ppermute | solution.py:15
  8.5 1.7 fusion.315
  16.2 1.3 collective-permute-start.3
  17.5 4.6 %collective-permute-start.2 = (bf16[64,1,64]{2,0,1:T(8,128)(2,1)S(1)}, bf16[64,1,64]{2,0,1:T(8,128)(2,1)S(1)}, u32[]{:S(2)}, u32[]{:S(2)}) collective-permute-start(bf16[64,1,64]{2,0,1:T(8,128)(2,1)S(1)} %get-tuple-element.239), channel_id=1, source_target_pairs={{0,1},{1,2},{2,3},{3,4},{4,5},{6,7},{7,8},{8,9},{9,10},{10,11},{12... | collective-permute-start | bytes 24584 | tf_op jit(solution)/shard_map/ppermute | solution.py:15
  26.5 1.5 fusion.225
  35.1 1.3 collective-permute-start.5
  36.4 4.8 %collective-permute-start.4 = (bf16[128,1,64]{0,2,1:T(8,128)(2,1)S(1)}, bf16[128,1,64]{0,2,1:T(8,128)(2,1)S(1)}, u32[]{:S(2)}, u32[]{:S(2)}) collective-permute-start(bf16[128,1,64]{0,2,1:T(8,128)(2,1)S(1)} %get-tuple-element.221), channel_id=1, source_target_pairs={{0,1},{1,2},{2,3},{3,4},{4,5},{6,7},{7,8},{8,9},{9,10},{10,11},{12... | collective-permute-start | bytes 49160 | tf_op jit(solution)/shard_map/ppermute | solution.py:15
  49.8 11.9 %collective-permute-start.6 = (f32[138240]{0:T(1024)S(1)}, f32[138240]{0:T(1024)S(1)}, u32[]{:S(2)}, u32[]{:S(2)}) collective-permute-start(f32[138240]{0:T(1024)S(1)} %bitcast.702), channel_id=1, source_target_pairs={{0,6},{6,0},{1,7},{7,1},{2,8},{8,2},{3,9},{9,3},{4,10},{10,4},{5,1... | collective-permute-start | bytes 1658888 | tf_op jit(solution)/shard_map/ppermute | solution.py:111
  61.8 1.6 collective-permute-done.6
  63.7 1.5 dynamic-slice_reduce_fusion
  65.3 1.9 %collective-permute-start.7 = (f32[69120]{0:T(1024)S(1)}, f32[69120]{0:T(1024)S(1)}, u32[]{:S(2)}, u32[]{:S(2)}) collective-permute-start(f32[69120]{0:T(1024)S(1)} %get-tuple-element.7), channel_id=1, source_target_pairs={{0,24},{24,0},{1,25},{25,1},{2,26},{26,2},{3,27},{27,3},{4,28},{28... | collective-permute-start | bytes 829448 | tf_op jit(solution)/shard_map/ppermute | solution.py:111
  68.0 7.1 %collective-permute-done.7 = f32[69120]{0:T(1024)S(1)} collective-permute-done((f32[69120]{0:T(1024)S(1)}, f32[69120]{0:T(1024)S(1)}, u32[]{:S(2)}, u32[]{:S(2)}) %collective-permute-start.7) | collective-permute-done | bytes 276512 | tf_op jit(solution)/shard_map/ppermute | solution.py:111
  75.2 1.3 collective-permute-start.9
  76.5 4.5 %collective-permute-start.8 = (bf16[64,1,256]{2,1,0:T(2,128)(2,1)S(1)}, bf16[64,1,256]{2,1,0:T(2,128)(2,1)S(1)}, u32[]{:S(2)}, u32[]{:S(2)}) collective-permute-start(bf16[64,1,256]{2,1,0:T(2,128)(2,1)S(1)} %get-tuple-element.106), channel_id=1, source_target_pairs={{0,1},{1,2},{2,3},{3,4},{4,5},{6,7},{7,8},{8,9},{9,10},{10,11},{12... | collective-permute-start | bytes 98312 | tf_op jit(solution)/shard_map/ppermute | solution.py:15
  83.4 21.8 %all-to-all-start = ((f32[192,1,360]{2,1,0:T(1,128)}), f32[192,1,360]{2,1,0:T(1,128)S(1)}, u32[]{:S(2)}, u32[]{:S(2)}) async-start(f32[192,1,360]{2,1,0:T(1,128)} %all_to_all.10), calls=%async_computation | async-start | bytes 589824 | tf_op jit(solution)/shard_map/all_to_all | solution.py:131
  106.4 1.4 fusion.56
  111.8 10.0 %all-to-all-done = f32[192,1,360]{2,1,0:T(1,128)S(1)} async-done(((f32[192,1,360]{2,1,0:T(1,128)}), f32[192,1,360]{2,1,0:T(1,128)S(1)}, u32[]{:S(2)}, u32[]{:S(2)}) %all-to-all-start) | async-done | bytes 276512 | tf_op jit(solution)/shard_map/all_to_all | solution.py:131
  122.8 1.6 reduce.6
  125.1 11.9 %all-to-all-start.1 = ((bf16[192,2,180]{2,1,0:T(2,128)(2,1)}), bf16[192,2,180]{2,1,0:T(2,128)(2,1)S(1)}, u32[]{:S(2)}, u32[]{:S(2)}) async-start(bf16[192,2,180]{2,1,0:T(2,128)(2,1)} %reshape.375), calls=%async_computation.1 | async-start | bytes 393216 | tf_op jit(solution)/shard_map/all_to_all | solution.py:134
  137.4 15.1 %all-to-all-done.1 = bf16[192,2,180]{2,1,0:T(2,128)(2,1)S(1)} async-done(((bf16[192,2,180]{2,1,0:T(2,128)(2,1)}), bf16[192,2,180]{2,1,0:T(2,128)(2,1)S(1)}, u32[]{:S(2)}, u32[]{:S(2)}) %all-to-all-start.1) | async-done | bytes 138272 | tf_op jit(solution)/shard_map/all_to_all | solution.py:134
  154.0 2.2 %collective-permute-start.10 = (bf16[69120]{0:T(1024)(128)(2,1)S(1)}, bf16[69120]{0:T(1024)(128)(2,1)S(1)}, u32[]{:S(2)}, u32[]{:S(2)}) collective-permute-start(bf16[69120]{0:T(1024)(128)(2,1)S(1)} %reshape.363), channel_id=1, source_target_pairs={{0,24},{24,0},{1,25},{25,1},{2,26},{26,2},{3,27},{27,3},{4,28},{28... | collective-permute-start | bytes 414728 | tf_op jit(solution)/shard_map/ppermute | solution.py:116
  156.4 3.4 %collective-permute-done.10 = bf16[69120]{0:T(1024)(128)(2,1)S(1)} collective-permute-done((bf16[69120]{0:T(1024)(128)(2,1)S(1)}, bf16[69120]{0:T(1024)(128)(2,1)S(1)}, u32[]{:S(2)}, u32[]{:S(2)}) %collective-permute-start.10) | collective-permute-done | bytes 138272 | tf_op jit(solution)/shard_map/ppermute | solution.py:116
  159.9 7.2 %collective-permute-start.11 = (bf16[138240]{0:T(1024)(128)(2,1)S(1)}, bf16[138240]{0:T(1024)(128)(2,1)S(1)}, u32[]{:S(2)}, u32[]{:S(2)}) collective-permute-start(bf16[138240]{0:T(1024)(128)(2,1)S(1)} %pad_maximum_fusion.11), channel_id=1, source_target_pairs={{0,6},{6,0},{1,7},{7,1},{2,8},{8,2},{3,9},{9,3},{4,10},{10,4},{5,1... | collective-permute-start | bytes 829448 | tf_op jit(solution)/shard_map/ppermute | solution.py:116
  (287 shorter events, 41.7 us)
Async XLA Ops:
  0.6 9.6 %copy-start = (bf16[3,3,3,64,128]{4,3,2,1,0:T(8,128)(2,1)S(1)}, bf16[3,3,3,64,128]{4,3,2,1,0:T(8,128)(2,1)}, u32[]{:S(2)}) copy-start(bf16[3,3,3,64,128]{4,3,2,1,0:T(8,128)(2,1)} %param.7) | copy-start | bytes 1327108
  0.6 9.6 %copy-start.1 = (bf16[3,3,3,32,64]{4,3,2,1,0:T(8,128)(2,1)S(1)}, bf16[3,3,3,32,64]{4,3,2,1,0:T(8,128)(2,1)}, u32[]{:S(2)}) copy-start(bf16[3,3,3,32,64]{4,3,2,1,0:T(8,128)(2,1)} %param.6) | copy-start | bytes 331780
  1.7 8.7 %collective-permute-start.1 = (bf16[32,1,256]{2,1,0:T(2,128)(2,1)S(1)}, bf16[32,1,256]{2,1,0:T(2,128)(2,1)S(1)}, u32[]{:S(2)}, u32[]{:S(2)}) collective-permute-start(bf16[32,1,256]{2,1,0:T(2,128)(2,1)S(1)} %get-tuple-element.149), channel_id=1, source_target_pairs={{1,0},{2,1},{3,2},{4,3},{5,4},{7,6},{8,7},{9,8},{10,9},{11,10},{13... | collective-permute-start | bytes 49160 | tf_op jit(solution)/shard_map/ppermute | solution.py:18
  3.0 7.4 %collective-permute-start = (bf16[32,1,256]{2,1,0:T(2,128)(2,1)S(1)}, bf16[32,1,256]{2,1,0:T(2,128)(2,1)S(1)}, u32[]{:S(2)}, u32[]{:S(2)}) collective-permute-start(bf16[32,1,256]{2,1,0:T(2,128)(2,1)S(1)} %get-tuple-element.150), channel_id=1, source_target_pairs={{0,1},{1,2},{2,3},{3,4},{4,5},{6,7},{7,8},{8,9},{9,10},{10,11},{12... | collective-permute-start | bytes 49160 | tf_op jit(solution)/shard_map/ppermute | solution.py:15
  8.5 17.9 %copy-start.16 = (pred[64]{0:T(512)(128)(4,1)}, pred[64]{0:T(512)(128)(4,1)S(1)}, u32[]{:S(2)}) copy-start(pred[64]{0:T(512)(128)(4,1)S(1)} %get-tuple-element.280) | copy-start | bytes 196
  8.5 17.9 %copy-start.22 = (pred[64]{0:T(512)(128)(4,1)}, pred[64]{0:T(512)(128)(4,1)S(1)}, u32[]{:S(2)}) copy-start(pred[64]{0:T(512)(128)(4,1)S(1)} %get-tuple-element.279) | copy-start | bytes 196
  16.2 10.2 %collective-permute-start.3 = (bf16[64,1,64]{2,0,1:T(8,128)(2,1)S(1)}, bf16[64,1,64]{2,0,1:T(8,128)(2,1)S(1)}, u32[]{:S(2)}, u32[]{:S(2)}) collective-permute-start(bf16[64,1,64]{2,0,1:T(8,128)(2,1)S(1)} %get-tuple-element.238), channel_id=1, source_target_pairs={{1,0},{2,1},{3,2},{4,3},{5,4},{7,6},{8,7},{9,8},{10,9},{11,10},{13... | collective-permute-start | bytes 24584 | tf_op jit(solution)/shard_map/ppermute | solution.py:18
  17.5 8.9 %collective-permute-start.2 = (bf16[64,1,64]{2,0,1:T(8,128)(2,1)S(1)}, bf16[64,1,64]{2,0,1:T(8,128)(2,1)S(1)}, u32[]{:S(2)}, u32[]{:S(2)}) collective-permute-start(bf16[64,1,64]{2,0,1:T(8,128)(2,1)S(1)} %get-tuple-element.239), channel_id=1, source_target_pairs={{0,1},{1,2},{2,3},{3,4},{4,5},{6,7},{7,8},{8,9},{9,10},{10,11},{12... | collective-permute-start | bytes 24584 | tf_op jit(solution)/shard_map/ppermute | solution.py:15
  33.5 7.8 %copy-start.17 = (pred[64]{0:T(512)(128)(4,1)S(1)}, pred[64]{0:T(512)(128)(4,1)}, u32[]{:S(2)}) copy-start(pred[64]{0:T(512)(128)(4,1)} %copy-done.16) | copy-start | bytes 196
  33.5 8.4 %copy-start.23 = (pred[64]{0:T(512)(128)(4,1)S(1)}, pred[64]{0:T(512)(128)(4,1)}, u32[]{:S(2)}) copy-start(pred[64]{0:T(512)(128)(4,1)} %copy-done.22) | copy-start | bytes 196
  33.5 8.4 %copy-start.25 = (pred[64]{0:T(512)(128)(4,1)S(1)}, pred[64]{0:T(512)(128)(4,1)}, u32[]{:S(2)}) copy-start(pred[64]{0:T(512)(128)(4,1)} %copy-done.24) | copy-start | bytes 196
  35.1 6.2 %collective-permute-start.5 = (bf16[128,1,64]{0,2,1:T(8,128)(2,1)S(1)}, bf16[128,1,64]{0,2,1:T(8,128)(2,1)S(1)}, u32[]{:S(2)}, u32[]{:S(2)}) collective-permute-start(bf16[128,1,64]{0,2,1:T(8,128)(2,1)S(1)} %get-tuple-element.220), channel_id=1, source_target_pairs={{1,0},{2,1},{3,2},{4,3},{5,4},{7,6},{8,7},{9,8},{10,9},{11,10},{13... | collective-permute-start | bytes 49160 | tf_op jit(solution)/shard_map/ppermute | solution.py:18
  36.4 5.5 %collective-permute-start.4 = (bf16[128,1,64]{0,2,1:T(8,128)(2,1)S(1)}, bf16[128,1,64]{0,2,1:T(8,128)(2,1)S(1)}, u32[]{:S(2)}, u32[]{:S(2)}) collective-permute-start(bf16[128,1,64]{0,2,1:T(8,128)(2,1)S(1)} %get-tuple-element.221), channel_id=1, source_target_pairs={{0,1},{1,2},{2,3},{3,4},{4,5},{6,7},{7,8},{8,9},{9,10},{10,11},{12... | collective-permute-start | bytes 49160 | tf_op jit(solution)/shard_map/ppermute | solution.py:15
  49.8 13.5 %collective-permute-start.6 = (f32[138240]{0:T(1024)S(1)}, f32[138240]{0:T(1024)S(1)}, u32[]{:S(2)}, u32[]{:S(2)}) collective-permute-start(f32[138240]{0:T(1024)S(1)} %bitcast.702), channel_id=1, source_target_pairs={{0,6},{6,0},{1,7},{7,1},{2,8},{8,2},{3,9},{9,3},{4,10},{10,4},{5,1... | collective-permute-start | bytes 1658888 | tf_op jit(solution)/shard_map/ppermute | solution.py:111
  65.3 9.8 %collective-permute-start.7 = (f32[69120]{0:T(1024)S(1)}, f32[69120]{0:T(1024)S(1)}, u32[]{:S(2)}, u32[]{:S(2)}) collective-permute-start(f32[69120]{0:T(1024)S(1)} %get-tuple-element.7), channel_id=1, source_target_pairs={{0,24},{24,0},{1,25},{25,1},{2,26},{26,2},{3,27},{27,3},{4,28},{28... | collective-permute-start | bytes 829448 | tf_op jit(solution)/shard_map/ppermute | solution.py:111
  75.2 30.1 %collective-permute-start.9 = (bf16[64,1,256]{2,1,0:T(2,128)(2,1)S(1)}, bf16[64,1,256]{2,1,0:T(2,128)(2,1)S(1)}, u32[]{:S(2)}, u32[]{:S(2)}) collective-permute-start(bf16[64,1,256]{2,1,0:T(2,128)(2,1)S(1)} %get-tuple-element.105), channel_id=1, source_target_pairs={{1,0},{2,1},{3,2},{4,3},{5,4},{7,6},{8,7},{9,8},{10,9},{11,10},{13... | collective-permute-start | bytes 98312 | tf_op jit(solution)/shard_map/ppermute | solution.py:18
  76.5 28.8 %collective-permute-start.8 = (bf16[64,1,256]{2,1,0:T(2,128)(2,1)S(1)}, bf16[64,1,256]{2,1,0:T(2,128)(2,1)S(1)}, u32[]{:S(2)}, u32[]{:S(2)}) collective-permute-start(bf16[64,1,256]{2,1,0:T(2,128)(2,1)S(1)} %get-tuple-element.106), channel_id=1, source_target_pairs={{0,1},{1,2},{2,3},{3,4},{4,5},{6,7},{7,8},{8,9},{9,10},{10,11},{12... | collective-permute-start | bytes 98312 | tf_op jit(solution)/shard_map/ppermute | solution.py:15
  81.0 24.2 %copy-start.15 = (pred[256]{0:T(512)(128)(4,1)S(1)}, pred[256]{0:T(512)(128)(4,1)}, u32[]{:S(2)}) copy-start(pred[256]{0:T(512)(128)(4,1)} %copy-done.14) | copy-start | bytes 772
  81.1 24.2 %copy-start.19 = (pred[256]{0:T(512)(128)(4,1)S(1)}, pred[256]{0:T(512)(128)(4,1)}, u32[]{:S(2)}) copy-start(pred[256]{0:T(512)(128)(4,1)} %copy-done.18) | copy-start | bytes 772
  81.1 24.2 %copy-start.21 = (pred[256]{0:T(512)(128)(4,1)S(1)}, pred[256]{0:T(512)(128)(4,1)}, u32[]{:S(2)}) copy-start(pred[256]{0:T(512)(128)(4,1)} %copy-done.20) | copy-start | bytes 772
  83.4 38.4 %all-to-all-start = ((f32[192,1,360]{2,1,0:T(1,128)}), f32[192,1,360]{2,1,0:T(1,128)S(1)}, u32[]{:S(2)}, u32[]{:S(2)}) async-start(f32[192,1,360]{2,1,0:T(1,128)} %all_to_all.10), calls=%async_computation | async-start | bytes 589824 | tf_op jit(solution)/shard_map/all_to_all | solution.py:131
  125.1 27.4 %all-to-all-start.1 = ((bf16[192,2,180]{2,1,0:T(2,128)(2,1)}), bf16[192,2,180]{2,1,0:T(2,128)(2,1)S(1)}, u32[]{:S(2)}, u32[]{:S(2)}) async-start(bf16[192,2,180]{2,1,0:T(2,128)(2,1)} %reshape.375), calls=%async_computation.1 | async-start | bytes 393216 | tf_op jit(solution)/shard_map/all_to_all | solution.py:134
  154.0 5.8 %collective-permute-start.10 = (bf16[69120]{0:T(1024)(128)(2,1)S(1)}, bf16[69120]{0:T(1024)(128)(2,1)S(1)}, u32[]{:S(2)}, u32[]{:S(2)}) collective-permute-start(bf16[69120]{0:T(1024)(128)(2,1)S(1)} %reshape.363), channel_id=1, source_target_pairs={{0,24},{24,0},{1,25},{25,1},{2,26},{26,2},{3,27},{27,3},{4,28},{28... | collective-permute-start | bytes 414728 | tf_op jit(solution)/shard_map/ppermute | solution.py:116
  159.9 8.4 %collective-permute-start.11 = (bf16[138240]{0:T(1024)(128)(2,1)S(1)}, bf16[138240]{0:T(1024)(128)(2,1)S(1)}, u32[]{:S(2)}, u32[]{:S(2)}) collective-permute-start(bf16[138240]{0:T(1024)(128)(2,1)S(1)} %pad_maximum_fusion.11), channel_id=1, source_target_pairs={{0,6},{6,0},{1,7},{7,1},{2,8},{8,2},{3,9},{9,3},{4,10},{10,4},{5,1... | collective-permute-start | bytes 829448 | tf_op jit(solution)/shard_map/ppermute | solution.py:116
  (18 other events, 40.5 us)

commit v3 on v1

--- a/solution.py
+++ b/solution.py
@@ -119,7 +119,7 @@
     return jnp.concatenate([first, second])
 
 
-def mean_terms(terms, samples):
+def mean_terms(terms, samples, rider):
     axes = ("y_high", "x_high", "z_high", "space")
     devices = 1
     for axis in axes:
@@ -130,6 +130,7 @@
     own = swap_add(jnp.pad(flat, (0, padded - total)), "core")
     own = swap_add(own, "x_low")
     own = swap_add(own, "y_low")
+    own, rider = lax.optimization_barrier((own, rider))
     pieces = lax.all_to_all(own.reshape(devices, -1), axes, 0, 0, tiled=True)
     piece = (pieces.sum(axis=0) / samples).astype(jnp.bfloat16)
     spread = jnp.broadcast_to(piece, (devices,) + piece.shape)
@@ -140,7 +141,7 @@
     for term in terms:
         results.append(gathered[start : start + term.size].reshape(term.shape))
         start += term.size
-    return tuple(results)
+    return tuple(results), rider
 
 
 def shards(activations, cotangent, weight_mid, weight_deep):
@@ -163,10 +164,10 @@
     spread = upsample_cube(back_pooled, matrix) * 0.125
     mid_grad = gelu_back(mid_pre, spread).astype(jnp.bfloat16)
     mid_terms = weight_terms(source_ext, mid_grad, row_count, col_count)
+    (grad_mid, grad_deep), mid_grad = mean_terms((mid_terms, deep_terms), samples, mid_grad)
     grad_input = conv_cube(extend(mid_grad, 1), flip_taps(weight_mid), row_count, col_count).astype(
         jnp.bfloat16
     )
-    grad_mid, grad_deep = mean_terms((mid_terms, deep_terms), samples)
     return (grad_input[None], grad_mid, grad_deep)
 
 

time: 194 us -> 177 us (0.912)
  local copies, waits for them, and re-layouts: 34 us -> 21.6 us
  waiting for transfers between devices: 47 us -> 43.4 us
  starting transfers between devices: 79.6 us -> 82.1 us
  other arithmetic: 18.2 us -> 16 us
    all_to_all x1, waiting for transfers between devices: 15.1 us -> 9.15 us  [mean_terms(): pieces = lax.all_to_all(own.reshape(devices, -1), axes, 0, 0, tiled=True)]
    another operation x9, local copies, waits for them, and re-layouts: 6.22 us -> 0.86 us  [conv_cube(): tap_block = kernel[depth_tap, row_tap].reshape(3 * chans_in, chans_out)]
    mul x4 -> x3, local copies, waits for them, and re-layouts: 2.86 us -> 0.54 us  [shards(): spread = upsample_cube(back_pooled, matrix) * 0.125]
    all_to_all x1, starting transfers between devices: 5.94 us -> 8.19 us  [mean_terms(): mine = lax.all_to_all(spread, axes, 0, 0, tiled=True).reshape(-1)]
  transfers between devices with their start and end apart: 16 -> 16, of which waited for: 6 -> 8; matrix products, arithmetic and copies ran while one was open for 15% -> 9% of each run, Pallas kernels for 0% -> 0%
where the time goes in v3:
time: 177 us; the launch traced here: 176 us
  starting transfers between devices  82.1 us (46%)
  waiting for transfers between devices  43.4 us (25%)
  local copies, waits for them, and re-layouts  21.6 us (12%)
  other arithmetic  16 us (9%)
  matrix products  10.4 us (6%)
  between operations  2.49 us (1%)
    all_to_all x1, starting transfers between devices, mean_terms(): pieces = lax.all_to_all(own.reshape(devices, -1), axes, 0, 0, tiled=True)  20.2 us
    ppermute x4, starting transfers between devices, extended(): lax.ppermute(lax.slice_in_dim(block, block.shape[dim] - width, None, axis...  19.4 us
    ppermute x3, starting transfers between devices, swap_add(): return own + lax.ppermute(other, axis, [(0, 1), (1, 0)])  15.8 us
    all_to_all x1, waiting for transfers between devices, mean_terms(): mine = lax.all_to_all(spread, axes, 0, 0, tiled=True).reshape(-1)  15.4 us
    ppermute x3, starting transfers between devices, swap_join(): theirs = lax.ppermute(part, axis, [(0, 1), (1, 0)])  13.3 us
    ppermute x3, waiting for transfers between devices, swap_add(): return own + lax.ppermute(other, axis, [(0, 1), (1, 0)])  12.5 us
    another operation x44, other arithmetic, tap_patches(): jnp.stack([shifted(planes, row_tap - 1, col_tap - 1, row_count, col_count...  11.9 us
    all_to_all x1, waiting for transfers between devices, mean_terms(): pieces = lax.all_to_all(own.reshape(devices, -1), axes, 0, 0, tiled=True)  9.15 us
  transfers between devices with their start and end apart: 16, of which 8 were waited for; matrix products, arithmetic and copies ran while one was open for 9% of the time, Pallas kernels for 0%

profile of v3, /device:TPU:1, one launch (start us, length us, event | category | flops | bytes accessed | tf_op | source)
XLA Modules:
  0.0 176.0 jit_solution(13341752721375229452)
XLA Ops:
  3.0 5.5 %collective-permute-start = (bf16[32,1,256]{2,1,0:T(2,128)(2,1)S(1)}, bf16[32,1,256]{2,1,0:T(2,128)(2,1)S(1)}, u32[]{:S(2)}, u32[]{:S(2)}) collective-permute-start(bf16[32,1,256]{2,1,0:T(2,128)(2,1)S(1)} %get-tuple-element.154), channel_id=1, source_target_pairs={{0,1},{1,2},{2,3},{3,4},{4,5},{6,7},{7,8},{8,9},{9,10},{10,11},{12... | collective-permute-start | bytes 49160 | tf_op jit(solution)/shard_map/ppermute | solution.py:15
  8.5 1.7 fusion.315
  17.5 4.6 %collective-permute-start.2 = (bf16[64,1,64]{2,0,1:T(8,128)(2,1)S(1)}, bf16[64,1,64]{2,0,1:T(8,128)(2,1)S(1)}, u32[]{:S(2)}, u32[]{:S(2)}) collective-permute-start(bf16[64,1,64]{2,0,1:T(8,128)(2,1)S(1)} %get-tuple-element.243), channel_id=1, source_target_pairs={{0,1},{1,2},{2,3},{3,4},{4,5},{6,7},{7,8},{8,9},{9,10},{10,11},{12... | collective-permute-start | bytes 24584 | tf_op jit(solution)/shard_map/ppermute | solution.py:15
  26.5 1.5 fusion.225
  36.4 4.8 %collective-permute-start.4 = (bf16[128,1,64]{0,2,1:T(8,128)(2,1)S(1)}, bf16[128,1,64]{0,2,1:T(8,128)(2,1)S(1)}, u32[]{:S(2)}, u32[]{:S(2)}) collective-permute-start(bf16[128,1,64]{0,2,1:T(8,128)(2,1)S(1)} %get-tuple-element.225), channel_id=1, source_target_pairs={{0,1},{1,2},{2,3},{3,4},{4,5},{6,7},{7,8},{8,9},{9,10},{10,11},{12... | collective-permute-start | bytes 49160 | tf_op jit(solution)/shard_map/ppermute | solution.py:15
  49.8 11.9 %collective-permute-start.6 = (f32[138240]{0:T(1024)S(1)}, f32[138240]{0:T(1024)S(1)}, u32[]{:S(2)}, u32[]{:S(2)}) collective-permute-start(f32[138240]{0:T(1024)S(1)} %bitcast.702), channel_id=1, source_target_pairs={{0,6},{6,0},{1,7},{7,1},{2,8},{8,2},{3,9},{9,3},{4,10},{10,4},{5,1... | collective-permute-start | bytes 1658888 | tf_op jit(solution)/shard_map/ppermute | solution.py:111
  61.8 1.6 collective-permute-done.6
  63.7 1.5 dynamic-slice_reduce_fusion
  65.2 1.9 %collective-permute-start.7 = (f32[69120]{0:T(1024)S(1)}, f32[69120]{0:T(1024)S(1)}, u32[]{:S(2)}, u32[]{:S(2)}) collective-permute-start(f32[69120]{0:T(1024)S(1)} %get-tuple-element.7), channel_id=1, source_target_pairs={{0,24},{24,0},{1,25},{25,1},{2,26},{26,2},{3,27},{27,3},{4,28},{28... | collective-permute-start | bytes 829448 | tf_op jit(solution)/shard_map/ppermute | solution.py:111
  67.6 7.4 %collective-permute-done.7 = f32[69120]{0:T(1024)S(1)} collective-permute-done((f32[69120]{0:T(1024)S(1)}, f32[69120]{0:T(1024)S(1)}, u32[]{:S(2)}, u32[]{:S(2)}) %collective-permute-start.7) | collective-permute-done | bytes 276512 | tf_op jit(solution)/shard_map/ppermute | solution.py:111
  76.0 1.9 %collective-permute-start.8 = (f32[34560]{0:T(1024)S(1)}, f32[34560]{0:T(1024)S(1)}, u32[]{:S(2)}, u32[]{:S(2)}) collective-permute-start(f32[34560]{0:T(1024)S(1)} %get-tuple-element.9), channel_id=1, source_target_pairs={{0,96},{96,0},{1,97},{97,1},{2,98},{98,2},{3,99},{99,3},{4,100},{1... | collective-permute-start | bytes 414728 | tf_op jit(solution)/shard_map/ppermute | solution.py:111
  78.3 3.5 %collective-permute-done.8 = f32[34560]{0:T(1024)S(1)} collective-permute-done((f32[34560]{0:T(1024)S(1)}, f32[34560]{0:T(1024)S(1)}, u32[]{:S(2)}, u32[]{:S(2)}) %collective-permute-start.8) | collective-permute-done | bytes 138272 | tf_op jit(solution)/shard_map/ppermute | solution.py:111
  82.0 1.3 collective-permute-start.10
  83.3 4.5 %collective-permute-start.9 = (bf16[64,1,256]{2,1,0:T(2,128)(2,1)S(1)}, bf16[64,1,256]{2,1,0:T(2,128)(2,1)S(1)}, u32[]{:S(2)}, u32[]{:S(2)}) collective-permute-start(bf16[64,1,256]{2,1,0:T(2,128)(2,1)S(1)} %get-tuple-element.110), channel_id=1, source_target_pairs={{0,1},{1,2},{2,3},{3,4},{4,5},{6,7},{7,8},{8,9},{9,10},{10,11},{12... | collective-permute-start | bytes 98312 | tf_op jit(solution)/shard_map/ppermute | solution.py:15
  89.9 20.2 %all-to-all-start = ((f32[96,1,360]{2,1,0:T(1,128)}), f32[96,1,360]{2,1,0:T(1,128)S(1)}, u32[]{:S(2)}, u32[]{:S(2)}) async-start(f32[96,1,360]{2,1,0:T(1,128)} %all_to_all.10), calls=%async_computation | async-start | bytes 294912 | tf_op jit(solution)/shard_map/all_to_all | solution.py:134
  111.2 1.4 fusion.56
  116.5 9.1 %all-to-all-done = f32[96,1,360]{2,1,0:T(1,128)S(1)} async-done(((f32[96,1,360]{2,1,0:T(1,128)}), f32[96,1,360]{2,1,0:T(1,128)S(1)}, u32[]{:S(2)}, u32[]{:S(2)}) %all-to-all-start) | async-done | bytes 138272 | tf_op jit(solution)/shard_map/all_to_all | solution.py:134
  128.2 8.2 %all-to-all-start.1 = ((bf16[96,2,180]{2,1,0:T(2,128)(2,1)}), bf16[96,2,180]{2,1,0:T(2,128)(2,1)S(1)}, u32[]{:S(2)}, u32[]{:S(2)}) async-start(bf16[96,2,180]{2,1,0:T(2,128)(2,1)} %reshape.381), calls=%async_computation.1 | async-start | bytes 196608 | tf_op jit(solution)/shard_map/all_to_all | solution.py:137
  136.6 15.4 %all-to-all-done.1 = bf16[96,2,180]{2,1,0:T(2,128)(2,1)S(1)} async-done(((bf16[96,2,180]{2,1,0:T(2,128)(2,1)}), bf16[96,2,180]{2,1,0:T(2,128)(2,1)S(1)}, u32[]{:S(2)}, u32[]{:S(2)}) %all-to-all-start.1) | async-done | bytes 69152 | tf_op jit(solution)/shard_map/all_to_all | solution.py:137
  152.8 2.3 %collective-permute-start.11 = (bf16[34560]{0:T(1024)(128)(2,1)S(1)}, bf16[34560]{0:T(1024)(128)(2,1)S(1)}, u32[]{:S(2)}, u32[]{:S(2)}) collective-permute-start(bf16[34560]{0:T(1024)(128)(2,1)S(1)} %reshape.367), channel_id=1, source_target_pairs={{0,96},{96,0},{1,97},{97,1},{2,98},{98,2},{3,99},{99,3},{4,100},{1... | collective-permute-start | bytes 207368 | tf_op jit(solution)/shard_map/ppermute | solution.py:116
  155.5 2.4 %collective-permute-done.11 = bf16[34560]{0:T(1024)(128)(2,1)S(1)} collective-permute-done((bf16[34560]{0:T(1024)(128)(2,1)S(1)}, bf16[34560]{0:T(1024)(128)(2,1)S(1)}, u32[]{:S(2)}, u32[]{:S(2)}) %collective-permute-start.11) | collective-permute-done | bytes 69152 | tf_op jit(solution)/shard_map/ppermute | solution.py:116
  157.9 2.2 %collective-permute-start.12 = (bf16[69120]{0:T(1024)(128)(2,1)S(1)}, bf16[69120]{0:T(1024)(128)(2,1)S(1)}, u32[]{:S(2)}, u32[]{:S(2)}) collective-permute-start(bf16[69120]{0:T(1024)(128)(2,1)S(1)} %pad_maximum_fusion.21), channel_id=1, source_target_pairs={{0,24},{24,0},{1,25},{25,1},{2,26},{26,2},{3,27},{27,3},{4,28},{28... | collective-permute-start | bytes 414728 | tf_op jit(solution)/shard_map/ppermute | solution.py:116
  160.3 3.4 %collective-permute-done.12 = bf16[69120]{0:T(1024)(128)(2,1)S(1)} collective-permute-done((bf16[69120]{0:T(1024)(128)(2,1)S(1)}, bf16[69120]{0:T(1024)(128)(2,1)S(1)}, u32[]{:S(2)}, u32[]{:S(2)}) %collective-permute-start.12) | collective-permute-done | bytes 138272 | tf_op jit(solution)/shard_map/ppermute | solution.py:116
  163.8 8.8 %collective-permute-start.13 = (bf16[138240]{0:T(1024)(128)(2,1)S(1)}, bf16[138240]{0:T(1024)(128)(2,1)S(1)}, u32[]{:S(2)}, u32[]{:S(2)}) collective-permute-start(bf16[138240]{0:T(1024)(128)(2,1)S(1)} %pad_maximum_fusion.11), channel_id=1, source_target_pairs={{0,6},{6,0},{1,7},{7,1},{2,8},{8,2},{3,9},{9,3},{4,10},{10,4},{5,1... | collective-permute-start | bytes 829448 | tf_op jit(solution)/shard_map/ppermute | solution.py:116
  (296 shorter events, 46.4 us)
Async XLA Ops:
  0.6 9.6 %copy-start = (bf16[3,3,3,64,128]{4,3,2,1,0:T(8,128)(2,1)S(1)}, bf16[3,3,3,64,128]{4,3,2,1,0:T(8,128)(2,1)}, u32[]{:S(2)}) copy-start(bf16[3,3,3,64,128]{4,3,2,1,0:T(8,128)(2,1)} %param.7) | copy-start | bytes 1327108
  0.6 9.6 %copy-start.1 = (bf16[3,3,3,32,64]{4,3,2,1,0:T(8,128)(2,1)S(1)}, bf16[3,3,3,32,64]{4,3,2,1,0:T(8,128)(2,1)}, u32[]{:S(2)}) copy-start(bf16[3,3,3,32,64]{4,3,2,1,0:T(8,128)(2,1)} %param.6) | copy-start | bytes 331780
  1.7 8.7 %collective-permute-start.1 = (bf16[32,1,256]{2,1,0:T(2,128)(2,1)S(1)}, bf16[32,1,256]{2,1,0:T(2,128)(2,1)S(1)}, u32[]{:S(2)}, u32[]{:S(2)}) collective-permute-start(bf16[32,1,256]{2,1,0:T(2,128)(2,1)S(1)} %get-tuple-element.153), channel_id=1, source_target_pairs={{1,0},{2,1},{3,2},{4,3},{5,4},{7,6},{8,7},{9,8},{10,9},{11,10},{13... | collective-permute-start | bytes 49160 | tf_op jit(solution)/shard_map/ppermute | solution.py:18
  3.0 7.4 %collective-permute-start = (bf16[32,1,256]{2,1,0:T(2,128)(2,1)S(1)}, bf16[32,1,256]{2,1,0:T(2,128)(2,1)S(1)}, u32[]{:S(2)}, u32[]{:S(2)}) collective-permute-start(bf16[32,1,256]{2,1,0:T(2,128)(2,1)S(1)} %get-tuple-element.154), channel_id=1, source_target_pairs={{0,1},{1,2},{2,3},{3,4},{4,5},{6,7},{7,8},{8,9},{9,10},{10,11},{12... | collective-permute-start | bytes 49160 | tf_op jit(solution)/shard_map/ppermute | solution.py:15
  8.5 17.9 %copy-start.16 = (pred[64]{0:T(512)(128)(4,1)}, pred[64]{0:T(512)(128)(4,1)S(1)}, u32[]{:S(2)}) copy-start(pred[64]{0:T(512)(128)(4,1)S(1)} %get-tuple-element.284) | copy-start | bytes 196
  8.5 17.9 %copy-start.22 = (pred[64]{0:T(512)(128)(4,1)}, pred[64]{0:T(512)(128)(4,1)S(1)}, u32[]{:S(2)}) copy-start(pred[64]{0:T(512)(128)(4,1)S(1)} %get-tuple-element.283) | copy-start | bytes 196
  16.2 10.1 %collective-permute-start.3 = (bf16[64,1,64]{2,0,1:T(8,128)(2,1)S(1)}, bf16[64,1,64]{2,0,1:T(8,128)(2,1)S(1)}, u32[]{:S(2)}, u32[]{:S(2)}) collective-permute-start(bf16[64,1,64]{2,0,1:T(8,128)(2,1)S(1)} %get-tuple-element.242), channel_id=1, source_target_pairs={{1,0},{2,1},{3,2},{4,3},{5,4},{7,6},{8,7},{9,8},{10,9},{11,10},{13... | collective-permute-start | bytes 24584 | tf_op jit(solution)/shard_map/ppermute | solution.py:18
  17.5 8.8 %collective-permute-start.2 = (bf16[64,1,64]{2,0,1:T(8,128)(2,1)S(1)}, bf16[64,1,64]{2,0,1:T(8,128)(2,1)S(1)}, u32[]{:S(2)}, u32[]{:S(2)}) collective-permute-start(bf16[64,1,64]{2,0,1:T(8,128)(2,1)S(1)} %get-tuple-element.243), channel_id=1, source_target_pairs={{0,1},{1,2},{2,3},{3,4},{4,5},{6,7},{7,8},{8,9},{9,10},{10,11},{12... | collective-permute-start | bytes 24584 | tf_op jit(solution)/shard_map/ppermute | solution.py:15
  33.5 8.4 %copy-start.23 = (pred[64]{0:T(512)(128)(4,1)S(1)}, pred[64]{0:T(512)(128)(4,1)}, u32[]{:S(2)}) copy-start(pred[64]{0:T(512)(128)(4,1)} %copy-done.22) | copy-start | bytes 196
  35.1 6.2 %collective-permute-start.5 = (bf16[128,1,64]{0,2,1:T(8,128)(2,1)S(1)}, bf16[128,1,64]{0,2,1:T(8,128)(2,1)S(1)}, u32[]{:S(2)}, u32[]{:S(2)}) collective-permute-start(bf16[128,1,64]{0,2,1:T(8,128)(2,1)S(1)} %get-tuple-element.224), channel_id=1, source_target_pairs={{1,0},{2,1},{3,2},{4,3},{5,4},{7,6},{8,7},{9,8},{10,9},{11,10},{13... | collective-permute-start | bytes 49160 | tf_op jit(solution)/shard_map/ppermute | solution.py:18
  36.4 5.5 %collective-permute-start.4 = (bf16[128,1,64]{0,2,1:T(8,128)(2,1)S(1)}, bf16[128,1,64]{0,2,1:T(8,128)(2,1)S(1)}, u32[]{:S(2)}, u32[]{:S(2)}) collective-permute-start(bf16[128,1,64]{0,2,1:T(8,128)(2,1)S(1)} %get-tuple-element.225), channel_id=1, source_target_pairs={{0,1},{1,2},{2,3},{3,4},{4,5},{6,7},{7,8},{8,9},{9,10},{10,11},{12... | collective-permute-start | bytes 49160 | tf_op jit(solution)/shard_map/ppermute | solution.py:15
  49.8 13.5 %collective-permute-start.6 = (f32[138240]{0:T(1024)S(1)}, f32[138240]{0:T(1024)S(1)}, u32[]{:S(2)}, u32[]{:S(2)}) collective-permute-start(f32[138240]{0:T(1024)S(1)} %bitcast.702), channel_id=1, source_target_pairs={{0,6},{6,0},{1,7},{7,1},{2,8},{8,2},{3,9},{9,3},{4,10},{10,4},{5,1... | collective-permute-start | bytes 1658888 | tf_op jit(solution)/shard_map/ppermute | solution.py:111
  65.2 9.8 %collective-permute-start.7 = (f32[69120]{0:T(1024)S(1)}, f32[69120]{0:T(1024)S(1)}, u32[]{:S(2)}, u32[]{:S(2)}) collective-permute-start(f32[69120]{0:T(1024)S(1)} %get-tuple-element.7), channel_id=1, source_target_pairs={{0,24},{24,0},{1,25},{25,1},{2,26},{26,2},{3,27},{27,3},{4,28},{28... | collective-permute-start | bytes 829448 | tf_op jit(solution)/shard_map/ppermute | solution.py:111
  76.0 5.8 %collective-permute-start.8 = (f32[34560]{0:T(1024)S(1)}, f32[34560]{0:T(1024)S(1)}, u32[]{:S(2)}, u32[]{:S(2)}) collective-permute-start(f32[34560]{0:T(1024)S(1)} %get-tuple-element.9), channel_id=1, source_target_pairs={{0,96},{96,0},{1,97},{97,1},{2,98},{98,2},{3,99},{99,3},{4,100},{1... | collective-permute-start | bytes 414728 | tf_op jit(solution)/shard_map/ppermute | solution.py:111
  81.8 28.3 %copy-start.15 = (pred[256]{0:T(512)(128)(4,1)S(1)}, pred[256]{0:T(512)(128)(4,1)}, u32[]{:S(2)}) copy-start(pred[256]{0:T(512)(128)(4,1)} %copy-done.14) | copy-start | bytes 772
  81.9 28.3 %copy-start.19 = (pred[256]{0:T(512)(128)(4,1)S(1)}, pred[256]{0:T(512)(128)(4,1)}, u32[]{:S(2)}) copy-start(pred[256]{0:T(512)(128)(4,1)} %copy-done.18) | copy-start | bytes 772
  81.9 28.3 %copy-start.21 = (pred[256]{0:T(512)(128)(4,1)S(1)}, pred[256]{0:T(512)(128)(4,1)}, u32[]{:S(2)}) copy-start(pred[256]{0:T(512)(128)(4,1)} %copy-done.20) | copy-start | bytes 772
  82.0 28.1 %collective-permute-start.10 = (bf16[64,1,256]{2,1,0:T(2,128)(2,1)S(1)}, bf16[64,1,256]{2,1,0:T(2,128)(2,1)S(1)}, u32[]{:S(2)}, u32[]{:S(2)}) collective-permute-start(bf16[64,1,256]{2,1,0:T(2,128)(2,1)S(1)} %get-tuple-element.109), channel_id=1, source_target_pairs={{1,0},{2,1},{3,2},{4,3},{5,4},{7,6},{8,7},{9,8},{10,9},{11,10},{13... | collective-permute-start | bytes 98312 | tf_op jit(solution)/shard_map/ppermute | solution.py:18
  83.3 26.8 %collective-permute-start.9 = (bf16[64,1,256]{2,1,0:T(2,128)(2,1)S(1)}, bf16[64,1,256]{2,1,0:T(2,128)(2,1)S(1)}, u32[]{:S(2)}, u32[]{:S(2)}) collective-permute-start(bf16[64,1,256]{2,1,0:T(2,128)(2,1)S(1)} %get-tuple-element.110), channel_id=1, source_target_pairs={{0,1},{1,2},{2,3},{3,4},{4,5},{6,7},{7,8},{8,9},{9,10},{10,11},{12... | collective-permute-start | bytes 98312 | tf_op jit(solution)/shard_map/ppermute | solution.py:15
  89.9 35.8 %all-to-all-start = ((f32[96,1,360]{2,1,0:T(1,128)}), f32[96,1,360]{2,1,0:T(1,128)S(1)}, u32[]{:S(2)}, u32[]{:S(2)}) async-start(f32[96,1,360]{2,1,0:T(1,128)} %all_to_all.10), calls=%async_computation | async-start | bytes 294912 | tf_op jit(solution)/shard_map/all_to_all | solution.py:134
  128.2 23.8 %all-to-all-start.1 = ((bf16[96,2,180]{2,1,0:T(2,128)(2,1)}), bf16[96,2,180]{2,1,0:T(2,128)(2,1)S(1)}, u32[]{:S(2)}, u32[]{:S(2)}) async-start(bf16[96,2,180]{2,1,0:T(2,128)(2,1)} %reshape.381), calls=%async_computation.1 | async-start | bytes 196608 | tf_op jit(solution)/shard_map/all_to_all | solution.py:137
  152.8 5.1 %collective-permute-start.11 = (bf16[34560]{0:T(1024)(128)(2,1)S(1)}, bf16[34560]{0:T(1024)(128)(2,1)S(1)}, u32[]{:S(2)}, u32[]{:S(2)}) collective-permute-start(bf16[34560]{0:T(1024)(128)(2,1)S(1)} %reshape.367), channel_id=1, source_target_pairs={{0,96},{96,0},{1,97},{97,1},{2,98},{98,2},{3,99},{99,3},{4,100},{1... | collective-permute-start | bytes 207368 | tf_op jit(solution)/shard_map/ppermute | solution.py:116
  157.9 5.8 %collective-permute-start.12 = (bf16[69120]{0:T(1024)(128)(2,1)S(1)}, bf16[69120]{0:T(1024)(128)(2,1)S(1)}, u32[]{:S(2)}, u32[]{:S(2)}) collective-permute-start(bf16[69120]{0:T(1024)(128)(2,1)S(1)} %pad_maximum_fusion.21), channel_id=1, source_target_pairs={{0,24},{24,0},{1,25},{25,1},{2,26},{26,2},{3,27},{27,3},{4,28},{28... | collective-permute-start | bytes 414728 | tf_op jit(solution)/shard_map/ppermute | solution.py:116
  163.8 10.1 %collective-permute-start.13 = (bf16[138240]{0:T(1024)(128)(2,1)S(1)}, bf16[138240]{0:T(1024)(128)(2,1)S(1)}, u32[]{:S(2)}, u32[]{:S(2)}) collective-permute-start(bf16[138240]{0:T(1024)(128)(2,1)S(1)} %pad_maximum_fusion.11), channel_id=1, source_target_pairs={{0,6},{6,0},{1,7},{7,1},{2,8},{8,2},{3,9},{9,3},{4,10},{10,4},{5,1... | collective-permute-start | bytes 829448 | tf_op jit(solution)/shard_map/ppermute | solution.py:116
  (20 other events, 56.7 us)
